TPU v7x, 256 devices: a whole 4x4x8 slice. The times are simulated.
256 devices in a mesh: member: 128 (over y, z_lo, x, core), mp: 2 (over z_hi).
Axes of the slice: x: 4, y: 4, z: 8 (z_hi: 2, z_lo: 4; z = z_hi * 4 + z_lo), core: 2. Of those that a mesh axis runs over, the one named last changes fastest.
Arguments:
- token_ids: int32 [512, 64], P('member'), may hold values from 0 to 76031
- fit_ranks: int32 [512], P('member'), may hold values from 0 to 511, as said below
- embed_table: bfloat16 [3584, 76032], P('member'), may hold values from -40 to 40
- norm_gain: float32 [3584], replicated, may hold values from 0.1 to 1.9
- qkv_weight: bfloat16 [3584, 2304], P('member', 'mp'), may hold values from -0.09375 to 0.09375
- qkv_bias: float32 [2304], P('mp'), may hold values from -3 to 3
- out_weight: bfloat16 [3584, 1792], P('member', 'mp'), may hold values from -0.125 to 0.125
- value_weight: float32 [3584], replicated, may hold values from -0.09375 to 0.09375
- qkv_left: bfloat16 [512, 3584], P('member'), may hold values from -5 to 5
- qkv_right: bfloat16 [512, 2304], P('member', 'mp'), may hold values from -5 to 5
- out_left: bfloat16 [512, 1792], P('member', 'mp'), may hold values from -5 to 5
- out_right: bfloat16 [512, 3584], P('member'), may hold values from -5 to 5
Outputs:
- values: float32 [512, 64], P(('member', 'mp'))
- qkv_grad: float32 [3584, 2304], P('member', 'mp')
- out_grad: float32 [3584, 1792], P('member', 'mp')
Inputs may be any that keep to these rules, and one draw needn't show every extreme that they name: `fit_ranks`: A member's rank is the number of members whose integer fitness score is strictly lower; equal scores share a rank.
All inputs are finite; a program needn't handle non-finite values.
Results may differ from a plain program's by a relative error of at most 0.0052.
Values may be sent and summed in bfloat16 or wider, within the bound.
No kernel may reach another device: no remote copies, remote signals or barrier semaphores. Data moves between devices by JAX's collectives and lax.ppermute only.
A program may use at most 128 MiB of HBM per device.

v0:
```python
import math

import jax
import jax.numpy as jnp
from jax import lax
from jax.sharding import PartitionSpec as P

HD = 128
HQ = 14
HK = 2


SIGMA = 0.01
EPSILON = 1e-06
THETA = 1000000.0
MASKED = -1e30


def rope_tables(length, head_size):
    halfway = head_size // 2
    inverse = THETA ** (-(jnp.arange(halfway, dtype=jnp.float32) * 2.0 / head_size))
    places = jnp.arange(length, dtype=jnp.float32)
    angles = places[:, None] * inverse[None, :]
    angles = jnp.concatenate([angles, angles], axis=1)
    return (jnp.cos(angles), jnp.sin(angles))


def rotate(states, cosine, sine_table):
    halfway = states.shape[-1] // 2
    turned = jnp.concatenate([-states[..., halfway:], states[..., :halfway]], axis=-1)
    return states * cosine[None, :, None, :] + turned * sine_table[None, :, None, :]


def attend(query_heads, key_heads, value_heads, kv_count):
    members, length, head_count, head_size = query_heads.shape
    group_size = head_count // kv_count
    grouped = query_heads.reshape(members, length, kv_count, group_size, head_size)
    scores = jnp.einsum(
        "mskgd,mtkd->mkgst", grouped, key_heads, preferred_element_type=jnp.float32
    ) / math.sqrt(head_size)
    causal = jnp.arange(length)[None, :] <= jnp.arange(length)[:, None]
    scores = jnp.where(causal, scores, MASKED)
    top = jnp.max(scores, axis=-1, keepdims=True)
    weights = jnp.exp(scores - top)
    weights = (weights / jnp.sum(weights, axis=-1, keepdims=True)).astype(jnp.bfloat16)
    context = jnp.einsum(
        "mkgst,mtkd->mskgd", weights, value_heads, preferred_element_type=jnp.float32
    )
    return context.astype(jnp.bfloat16).reshape(members, length, head_count * head_size)


def on_device(
    token_ids,
    fit_ranks,
    embed_table,
    norm_gain,
    qkv_weight,
    qkv_bias,
    out_weight,
    value_weight,
    qkv_left,
    qkv_right,
    out_left,
    out_right,
):
    members, length = token_ids.shape
    row_count = members * length
    mp_size = lax.axis_size("mp")
    heads_here = HQ // mp_size
    kv_here = HK // mp_size
    population = members * lax.axis_size("member")
    contract_rows = (((0,), (0,)), ((), ()))
    contract_cols = (((1,), (1,)), ((), ()))
    all_ids = lax.all_gather(token_ids, "member", axis=0, tiled=True)
    picked = jnp.take(embed_table, all_ids.reshape(-1), axis=1)
    embedded = lax.all_to_all(picked, "member", split_axis=1, concat_axis=0, tiled=True)
    features = embedded.astype(jnp.float32)
    inverse_rms = lax.rsqrt(jnp.mean(features * features, axis=0, keepdims=True) + EPSILON)
    normed = (features * inverse_rms * norm_gain[:, None]).astype(jnp.bfloat16)
    base_proj = lax.dot_general(
        normed,
        lax.all_gather(qkv_weight, "member", axis=0, tiled=True),
        contract_rows,
        preferred_element_type=jnp.float32,
    )
    normed_members = normed.reshape(normed.shape[0], members, length)
    coef_in = jnp.einsum("dms,md->ms", normed_members, qkv_left, preferred_element_type=jnp.float32)
    projected = (
        base_proj.reshape(members, length, -1)
        + SIGMA * coef_in[:, :, None] * qkv_right.astype(jnp.float32)[:, None, :]
        + qkv_bias[None, None, :]
    )
    query_width = heads_here * HD
    kv_width = kv_here * HD
    cosine, sine_table = rope_tables(length, HD)
    query_heads = rotate(
        projected[:, :, :query_width].reshape(members, length, heads_here, HD), cosine, sine_table
    ).astype(jnp.bfloat16)
    key_heads = rotate(
        projected[:, :, query_width : query_width + kv_width].reshape(members, length, kv_here, HD),
        cosine,
        sine_table,
    ).astype(jnp.bfloat16)
    value_heads = (
        projected[:, :, query_width + kv_width :]
        .reshape(members, length, kv_here, HD)
        .astype(jnp.bfloat16)
    )
    context = attend(query_heads, key_heads, value_heads, kv_here)
    coef_out = jnp.einsum("msq,mq->ms", context, out_left, preferred_element_type=jnp.float32)
    flat_context = context.reshape(row_count, query_width)
    share_rows = row_count // mp_size
    partial_out = lax.dot_general(
        flat_context,
        lax.all_gather(out_weight, "member", axis=0, tiled=True),
        contract_cols,
        preferred_element_type=jnp.float32,
    )
    head_term = (
        partial_out.reshape(members, length, -1)
        + SIGMA * coef_out[:, :, None] * out_right.astype(jnp.float32)[:, None, :]
    )
    summed = lax.psum_scatter(
        head_term.reshape(row_count, -1), "mp", scatter_dimension=0, tiled=True
    )
    mp_index = lax.axis_index("mp")
    own_embed = lax.dynamic_slice_in_dim(embedded, mp_index * share_rows, share_rows, 1)
    residual = own_embed.T.astype(jnp.float32) + summed
    inverse_out = lax.rsqrt(jnp.mean(residual * residual, axis=1, keepdims=True) + EPSILON)
    value_rows = jnp.sum(residual * inverse_out * value_weight[None, :], axis=1).reshape(
        members // mp_size, length
    )
    rank_values = fit_ranks.astype(jnp.float32)
    first_sum, second_sum = lax.psum(
        (jnp.sum(rank_values), jnp.sum(rank_values * rank_values)), "member"
    )
    center = first_sum / population
    spread = second_sum / population - center * center
    fit_local = (rank_values - center) * lax.rsqrt(spread + EPSILON)
    fitness = lax.all_gather(fit_local, "member", axis=0, tiled=True)
    left_rows, right_rows = (
        lax.all_to_all(qkv_left, "member", split_axis=1, concat_axis=0, tiled=True),
        lax.all_to_all(out_right, "member", split_axis=1, concat_axis=0, tiled=True),
    )
    right_cols, left_cols = (
        lax.all_gather(qkv_right, "member", axis=0, tiled=True),
        lax.all_gather(out_left, "member", axis=0, tiled=True),
    )
    weighted_in = left_rows.astype(jnp.float32) * fitness[:, None]
    qkv_grad = lax.dot_general(
        weighted_in,
        right_cols.astype(jnp.float32),
        contract_rows,
        precision=lax.Precision.HIGHEST,
        preferred_element_type=jnp.float32,
    ) / (population * SIGMA)
    weighted_out = right_rows.astype(jnp.float32) * fitness[:, None]
    out_grad = lax.dot_general(
        weighted_out,
        left_cols.astype(jnp.float32),
        contract_rows,
        precision=lax.Precision.HIGHEST,
        preferred_element_type=jnp.float32,
    ) / (population * SIGMA)
    return (value_rows, qkv_grad, out_grad)


def solution(mesh):
    placed = (
        P("member", None),
        P("member"),
        P("member", None),
        P(),
        P("member", "mp"),
        P("mp"),
        P("member", "mp"),
        P(),
        P("member", None),
        P("member", "mp"),
        P("member", "mp"),
        P("member", None),
    )
    return jax.shard_map(
        on_device,
        mesh=mesh,
        in_specs=placed,
        out_specs=(P(("member", "mp"), None), P("member", "mp"), P("member", "mp")),
        check_vma=False,
    )
```

profile of v0, /device:TPU:1, one launch (start us, length us, event | category | flops | bytes accessed | tf_op | source)
XLA Modules:
  0.0 1389.6 jit_solution(669175354803693460)
XLA Ops:
  7.2 0.7 all-gather.11.cloned.1.call-update
  7.9 0.7 all-gather.9.cloned.1.call-update
  8.6 191.3 %all-gather = s32[128,4,64]{2,1,0:T(4,128)S(1)} all-gather(s32[1,4,64]{2,1,0:T(4,128)} %bitcast.92), channel_id=1, replica_groups=mesh['member'=128,'mp'=2] {'member'}, dimensions={0}, use_global_device_ids=true | all-gather | bytes 132096 | tf_op jit(solution)/shard_map/all_gather | solution.py:74
  200.3 15.7 %copy.45 = bf16[28,76032]{0,1:T(8,128)(2,1)} copy(bf16[28,76032]{1,0:T(8,128)(2,1)} %param.14) | data formatting | bytes 8515584 | tf_op args[2]
  216.1 118.4 %gather_fusion = bf16[32768,28]{1,0:T(8,128)(2,1)} fusion(bf16[28,76032]{0,1:T(8,128)(2,1)} %copy.45, s32[32768]{0:T(1024)S(1)} %broadcast_clamp_fusion), kind=kCustom, calls=%fused_computation | custom fusion | bytes 3801088 | tf_op jit(solution)/shard_map/jit(_take)/gather | solution.py:75
  334.5 7.6 copy.46
  342.3 1.6 broadcast_select_fusion
  343.9 5.5 all-to-all-start
  349.5 0.7 all-gather.13.cloned.1.call-update
  351.1 50.3 %all-to-all-done = bf16[28,128,256]{2,0,1:T(8,128)(2,1)S(1)} async-done(((bf16[28,128,256]{2,0,1:T(8,128)(2,1)}), bf16[28,128,256]{2,0,1:T(8,128)(2,1)S(1)}, u32[]{:S(2)}, u32[]{:S(2)}) %all-to-all-start) | async-done | bytes 1835040 | tf_op jit(solution)/shard_map/all_to_all | solution.py:76
  401.4 1.5 all_to_all.34
  403.6 3.7 fusion.3
  407.3 3.9 copy.47
  411.2 2.4 bitcast_convert_fusion
  413.7 7.7 reshape.204
  421.4 11.5 multiply_convert_fusion
  433.5 10.4 reshape.237
  444.0 12.7 reshape.232
  456.7 5.9 fusion.2
  465.9 6.8 convolution_add_fusion
  472.7 5.1 copy.51
  478.2 0.8 copy.53
  478.9 13.5 all-to-all-start.2
  492.4 199.5 %all-gather.4 = bf16[128,4,896]{2,1,0:T(4,128)(2,1)S(1)} all-gather(bf16[1,4,896]{2,1,0:T(4,128)(2,1)S(1)} %bitcast.91), channel_id=1, replica_groups=mesh['member'=128,'mp'=2] {'member'}, dimensions={0}, use_global_device_ids=true | all-gather | bytes 924672 | tf_op jit(solution)/shard_map/all_gather | solution.py:147
  692.5 337.3 %all-reduce.1 = (f32[]{:T(128)}, f32[]{:T(128)}) all-reduce(f32[]{:T(128)} %get-tuple-element.4, f32[]{:T(128)} %get-tuple-element.3), channel_id=1, replica_groups=mesh['member'=128,'mp'=2] {'member'}, use_global_device_ids=true, to_apply=%region_9.10 | all-reduce | flops 2 | bytes 16 | tf_op jit(solution)/shard_map/psum | solution.py:134
  1032.8 0.8 copy.52
  1034.9 5.3 all-to-all-start.1
  1040.5 333.7 %all-reduce = f32[512]{0:T(512)S(1)} all-reduce(f32[512]{0:T(512)S(1)} %multiply_dynamic-update-slice_fusion), channel_id=1, replica_groups=mesh['member'=128,'mp'=2] {'member'}, use_global_device_ids=true, to_apply=%add | all-reduce | flops 512 | bytes 4096
  1374.3 1.3 convolution_multiply_fusion.2
  1375.7 2.5 reshape.225
  1378.2 1.5 convolution_multiply_fusion
  1379.7 2.1 multiply_reduce_fusion.2
  (79 shorter events, 9.7 us)
Async XLA Ops:
  7.2 426.4 %all-gather.11.cloned.1.call-start = ((), (), s32[]{:S(2)}) async-start(), calls=%async_computation.6 | async-start | bytes 7397376 | tf_op jit(solution)/shard_map/all_gather | solution.py:115
  7.9 436.1 %all-gather.9.cloned.1.call-start = ((), (), s32[]{:S(2)}) async-start(), calls=%async_computation.5 | async-start | bytes 9510912 | tf_op jit(solution)/shard_map/all_gather | solution.py:82
  343.9 6.3 copy-start.6
  343.9 6.4 copy-start.3
  343.9 57.5 %all-to-all-start = ((bf16[28,128,256]{2,0,1:T(8,128)(2,1)}), bf16[28,128,256]{2,0,1:T(8,128)(2,1)S(1)}, u32[]{:S(2)}, u32[]{:S(2)}) async-start(bf16[28,128,256]{2,0,1:T(8,128)(2,1)} %broadcast_select_fusion), calls=%async_computation | async-start | bytes 4194304 | tf_op jit(solution)/shard_map/all_to_all | solution.py:76
  349.4 1026.3 %all-gather.13.cloned.1.call-start = ((), (), s32[]{:S(2)}) async-start(), calls=%async_computation.7 | async-start | bytes 1188864 | tf_op jit(solution)/shard_map/all_gather | solution.py:146
  350.2 1029.5 %reduce-scatter.2.cloned.1.call-start = ((), (), s32[]{:S(2)}) async-start(), calls=%async_computation.4 | async-start | bytes 5505024 | tf_op jit(solution)/shard_map/reduce_scatter | solution.py:123
  401.4 2.2 copy-start.4
  421.4 11.5 copy-start.7
  444.0 12.7 copy-start.2
  444.0 12.7 copy-start.11
  464.4 1.2 copy-start.9
  464.8 1.1 copy-start.5
  477.8 214.1 %copy-start.10 = (s32[4]{0:T(128)S(1)}, s32[4]{0:T(128)}, u32[]{:S(2)}) copy-start(s32[4]{0:T(128)} %param.13) | copy-start | bytes 52
  477.8 555.8 %copy-start.12 = (u32[256]{0:T(256)S(1)}, u32[256]{0:T(256)}, u32[]{:S(2)}) copy-start(u32[256]{0:T(256)} %constant.74) | copy-start | bytes 3076
  478.9 555.9 %all-to-all-start.2 = ((bf16[4,128,28]{2,0,1:T(4,128)(2,1)}), bf16[4,128,28]{2,0,1:T(4,128)(2,1)S(1)}, u32[]{:S(2)}, u32[]{:S(2)}) async-start(bf16[4,128,28]{2,0,1:T(4,128)(2,1)} %copy.53), calls=%async_computation.3 | async-start | bytes 262144 | tf_op jit(solution)/shard_map/all_to_all | solution.py:143
  1034.9 339.4 %all-to-all-start.1 = ((bf16[4,128,28]{2,0,1:T(4,128)(2,1)}), bf16[4,128,28]{2,0,1:T(4,128)(2,1)S(1)}, u32[]{:S(2)}, u32[]{:S(2)}) async-start(bf16[4,128,28]{2,0,1:T(4,128)(2,1)} %copy.52), calls=%async_computation.2 | async-start | bytes 262144 | tf_op jit(solution)/shard_map/all_to_all | solution.py:142
  1375.7 4.0 copy-start
  1378.2 3.6 copy-start.8
  1379.7 2.1 copy-start.1
Sparse Core Ops, SparseCore 0:
  9.8 207.3 all-gather.10
  219.1 217.1 all-gather.8
  438.1 197.6 all-gather.12
  638.2 97.2 reduce-scatter.1
where the time goes:
time: 1400 us; the launch traced here: 1390 us
  blocking collectives  1060 us (76%)
  local copies, waits for them, and re-layouts  191 us (14%)
  waiting for transfers between devices  52.4 us (4%)
  other arithmetic  25.4 us (2%)
  starting transfers between devices  24.5 us (2%)
  between operations  17.4 us (1%)
  matrix products  17.2 us (1%)
    psum x1, blocking collectives, on_device(): lax.psum((jnp.sum(rank_values), jnp.sum(rank_values * rank_values)), 'mem...  337 us
    unnamed x1, blocking collectives  334 us
    all_gather x1, blocking collectives, on_device(): lax.all_gather(out_left, 'member', axis=0, tiled=True)  200 us
    all_gather x1, blocking collectives, on_device(): all_ids = lax.all_gather(token_ids, 'member', axis=0, tiled=True)  191 us
    gather x2, local copies, waits for them, and re-layouts, on_device(): picked = jnp.take(embed_table, all_ids.reshape(-1), axis=1)  126 us
    all_to_all x1, waiting for transfers between devices, on_device(): lax.all_to_all(picked, 'member', split_axis=1, concat_axis=0, tiled=True)  50.3 us
    unnamed x33, local copies, waits for them, and re-layouts  42.2 us
  transfers between devices with their start and end apart: 7, of which 1 were waited for; matrix products, arithmetic and copies ran while one was open for 16% of the time, Pallas kernels for 0%

commit v1 on v0

--- a/solution.py
+++ b/solution.py
@@ -71,7 +71,26 @@
     population = members * lax.axis_size("member")
     contract_rows = (((0,), (0,)), ((), ()))
     contract_cols = (((1,), (1,)), ((), ()))
-    all_ids = lax.all_gather(token_ids, "member", axis=0, tiled=True)
+    member_count = lax.axis_size("member")
+    packed_ids = jnp.concatenate([token_ids, fit_ranks[:, None]], axis=1)
+    spread_ids = jnp.broadcast_to(packed_ids[None], (member_count,) + packed_ids.shape)
+    every_ids = lax.all_to_all(spread_ids, "member", split_axis=0, concat_axis=0, tiled=True)
+    all_ids = every_ids[:, :, :length].reshape(population, length)
+    all_ranks = every_ids[:, :, length].reshape(population)
+    feature_rows = qkv_weight.shape[0]
+    qkv_cols = qkv_weight.shape[1]
+    stacked = jnp.concatenate(
+        [
+            jnp.concatenate([qkv_weight, out_weight], axis=1),
+            jnp.concatenate([qkv_right, out_left], axis=1),
+        ],
+        axis=0,
+    )
+    gathered = lax.all_gather(stacked, "member", axis=0)
+    full_qkv = gathered[:, :feature_rows, :qkv_cols].reshape(-1, qkv_cols)
+    full_out = gathered[:, :feature_rows, qkv_cols:].reshape(-1, out_weight.shape[1])
+    right_cols = gathered[:, feature_rows:, :qkv_cols].reshape(population, qkv_cols)
+    left_cols = gathered[:, feature_rows:, qkv_cols:].reshape(population, out_left.shape[1])
     picked = jnp.take(embed_table, all_ids.reshape(-1), axis=1)
     embedded = lax.all_to_all(picked, "member", split_axis=1, concat_axis=0, tiled=True)
     features = embedded.astype(jnp.float32)
@@ -79,7 +98,7 @@
     normed = (features * inverse_rms * norm_gain[:, None]).astype(jnp.bfloat16)
     base_proj = lax.dot_general(
         normed,
-        lax.all_gather(qkv_weight, "member", axis=0, tiled=True),
+        full_qkv,
         contract_rows,
         preferred_element_type=jnp.float32,
     )
@@ -112,7 +131,7 @@
     share_rows = row_count // mp_size
     partial_out = lax.dot_general(
         flat_context,
-        lax.all_gather(out_weight, "member", axis=0, tiled=True),
+        full_out,
         contract_cols,
         preferred_element_type=jnp.float32,
     )
@@ -130,22 +149,20 @@
     value_rows = jnp.sum(residual * inverse_out * value_weight[None, :], axis=1).reshape(
         members // mp_size, length
     )
-    rank_values = fit_ranks.astype(jnp.float32)
-    first_sum, second_sum = lax.psum(
-        (jnp.sum(rank_values), jnp.sum(rank_values * rank_values)), "member"
-    )
-    center = first_sum / population
-    spread = second_sum / population - center * center
-    fit_local = (rank_values - center) * lax.rsqrt(spread + EPSILON)
-    fitness = lax.all_gather(fit_local, "member", axis=0, tiled=True)
-    left_rows, right_rows = (
-        lax.all_to_all(qkv_left, "member", split_axis=1, concat_axis=0, tiled=True),
-        lax.all_to_all(out_right, "member", split_axis=1, concat_axis=0, tiled=True),
-    )
-    right_cols, left_cols = (
-        lax.all_gather(qkv_right, "member", axis=0, tiled=True),
-        lax.all_gather(out_left, "member", axis=0, tiled=True),
-    )
+    rank_values = all_ranks.astype(jnp.float32)
+    center = jnp.sum(rank_values) / population
+    spread = jnp.sum(rank_values * rank_values) / population - center * center
+    fitness = (rank_values - center) * lax.rsqrt(spread + EPSILON)
+    factor_rows = jnp.concatenate(
+        [
+            qkv_left.reshape(members, member_count, feature_rows),
+            out_right.reshape(members, member_count, feature_rows),
+        ],
+        axis=2,
+    )
+    factor_cols = lax.all_to_all(factor_rows, "member", split_axis=1, concat_axis=0, tiled=True)
+    left_rows = factor_cols[:, 0, :feature_rows]
+    right_rows = factor_cols[:, 0, feature_rows:]
     weighted_in = left_rows.astype(jnp.float32) * fitness[:, None]
     qkv_grad = lax.dot_general(
         weighted_in,

time: 1400 us -> 447 us (0.32)
  blocking collectives: 1060 us -> 0 us
  waiting for transfers between devices: 52.4 us -> 126 us
  local copies, waits for them, and re-layouts: 191 us -> 213 us
  starting transfers between devices: 24.5 us -> 40.3 us
    all_gather x2 -> x0, blocking collectives: 391 us -> none  [the longest x1 200 us: on_device(): lax.all_gather(out_left, 'member', axis=0, tiled=True)]
    psum x1 -> x0, blocking collectives: 337 us -> none  [on_device(): lax.psum((jnp.sum(rank_values), jnp.sum(rank_values * rank_values)), 'mem...]
    unnamed x1 -> x0, blocking collectives: 334 us -> none
    all_to_all x2, waiting for transfers between devices: 0.01 us -> 76.5 us  [the longest x1 76.5 us: on_device(): lax.all_to_all(factor_rows, 'member', split_axis=1, concat_axis=0, tiled=...]
    reshape x1 -> x6, local copies, waits for them, and re-layouts: 0.24 us -> 26.6 us  [the longest x1 12.7 us: on_device(): full_qkv = gathered[:, :feature_rows, :qkv_cols].reshape(-1, qkv_cols)]
    unnamed x33 -> x36, local copies, waits for them, and re-layouts: 42.2 us -> 17.1 us
    slice x0 -> x4, local copies, waits for them, and re-layouts: none -> 19.8 us  [the longest x1 8.03 us: on_device(): full_qkv = gathered[:, :feature_rows, :qkv_cols].reshape(-1, qkv_cols)]
  transfers between devices with their start and end apart: 7 -> 5, of which waited for: 1 -> 2; matrix products, arithmetic and copies ran while one was open for 16% -> 44% of each run, Pallas kernels for 0% -> 0%
where the time goes in v1:
time: 447 us; the launch traced here: 445 us
  local copies, waits for them, and re-layouts  213 us (48%)
  waiting for transfers between devices  126 us (28%)
  starting transfers between devices  40.3 us (9%)
  other arithmetic  29.6 us (7%)
  matrix products  18.4 us (4%)
  between operations  17 us (4%)
    gather x2, local copies, waits for them, and re-layouts, on_device(): picked = jnp.take(embed_table, all_ids.reshape(-1), axis=1)  126 us
    all_to_all x1, waiting for transfers between devices, on_device(): lax.all_to_all(factor_rows, 'member', split_axis=1, concat_axis=0, tiled=...  76.5 us
    all_to_all x1, waiting for transfers between devices, on_device(): lax.all_to_all(picked, 'member', split_axis=1, concat_axis=0, tiled=True)  49.5 us
    unnamed x36, local copies, waits for them, and re-layouts  17.1 us
    all_to_all x1, starting transfers between devices, on_device(): lax.all_to_all(factor_rows, 'member', split_axis=1, concat_axis=0, tiled=...  14.4 us
    all_to_all x1, starting transfers between devices, on_device(): lax.all_to_all(spread_ids, 'member', split_axis=0, concat_axis=0, tiled=T...  13.8 us
    reshape x1, local copies, waits for them, and re-layouts, on_device(): full_qkv = gathered[:, :feature_rows, :qkv_cols].reshape(-1, qkv_cols)  12.7 us
    all_to_all x1, starting transfers between devices, on_device(): lax.all_to_all(picked, 'member', split_axis=1, concat_axis=0, tiled=True)  11.8 us
  transfers between devices with their start and end apart: 5, of which 2 were waited for; matrix products, arithmetic and copies ran while one was open for 44% of the time, Pallas kernels for 0%

profile of v1, /device:TPU:1, one launch (start us, length us, event | category | flops | bytes accessed | tf_op | source)
XLA Modules:
  0.0 444.6 jit_solution(9038657335820391108)
XLA Ops:
  7.2 1.6 maximum_maximum_fusion
  11.1 13.8 %all-to-all-start = ((s32[128,4,65]{2,1,0:T(4,128)}), s32[128,4,65]{2,1,0:T(4,128)S(1)}, u32[]{:S(2)}, u32[]{:S(2)}) async-start(s32[128,4,65]{2,1,0:T(4,128)} %broadcast_in_dim.21), calls=%async_computation | async-start | bytes 524288 | tf_op jit(solution)/shard_map/all_to_all | solution.py:77
  24.9 15.7 %copy.64 = bf16[28,76032]{0,1:T(8,128)(2,1)} copy(bf16[28,76032]{1,0:T(8,128)(2,1)} %param.14) | data formatting | bytes 8515584 | tf_op args[2]
  41.2 118.6 %gather_fusion = bf16[32768,28]{1,0:T(8,128)(2,1)} fusion(bf16[28,76032]{0,1:T(8,128)(2,1)} %copy.64, s32[32768]{0:T(1024)S(1)} %broadcast_clamp_fusion), kind=kCustom, calls=%fused_computation | custom fusion | bytes 3801088 | tf_op jit(solution)/shard_map/jit(_take)/gather | solution.py:94
  159.8 7.6 %copy.65 = bf16[28,128,256]{2,0,1:T(8,128)(2,1)S(1)} copy(bf16[28,128,256]{0,2,1:T(8,128)(2,1)} %bitcast.86) | data formatting | bytes 3670016 | tf_op jit(solution)/shard_map/jit(_take)/gather | solution.py:94
  167.6 1.6 broadcast_select_fusion
  169.2 11.8 %all-to-all-start.1 = ((bf16[28,128,256]{2,0,1:T(8,128)(2,1)}), bf16[28,128,256]{2,0,1:T(8,128)(2,1)S(1)}, u32[]{:S(2)}, u32[]{:S(2)}) async-start(bf16[28,128,256]{2,0,1:T(8,128)(2,1)} %broadcast_select_fusion), calls=%async_computation.1 | async-start | bytes 4194304 | tf_op jit(solution)/shard_map/all_to_all | solution.py:95
  182.6 0.8 fusion.34
  183.4 49.5 %all-to-all-done.1 = bf16[28,128,256]{2,0,1:T(8,128)(2,1)S(1)} async-done(((bf16[28,128,256]{2,0,1:T(8,128)(2,1)}), bf16[28,128,256]{2,0,1:T(8,128)(2,1)S(1)}, u32[]{:S(2)}, u32[]{:S(2)}) %all-to-all-start.1) | async-done | bytes 1835040 | tf_op jit(solution)/shard_map/all_to_all | solution.py:95
  232.9 1.5 all_to_all.31
  235.0 3.7 fusion.3
  238.7 3.9 copy.66
  242.6 2.6 bitcast_convert_fusion
  245.2 7.7 %reshape.237 = f32[3584,4,64]{2,1,0:T(4,128)} reshape(f32[128,28,256]{2,1,0:T(8,128)} %bitcast_convert_fusion) | data formatting | bytes 7340032 | tf_op jit(solution)/shard_map/convert_element_type | solution.py:96
  252.9 11.5 %multiply_convert_fusion = bf16[3584,4,64]{2,1,0:T(4,128)(2,1)S(1)} fusion(f32[3584,4,64]{2,1,0:T(4,128)} %reshape.237, f32[3584]{0:T(1024)S(1)} %copy-done.8, f32[4,64]{1,0:T(4,128)S(1)} %rsqrt.24), kind=kLoop, calls=%fused_computation.1 | loop fusion | flops 2752512 | bytes 5520384 | tf_op jit(solution)/shard_map/convert_element_type | solution.py:98
  265.1 8.0 %slice.64 = bf16[128,28,1152]{2,1,0:T(8,128)(2,1)} slice(bf16[128,32,2048]{2,1,0:T(8,128)(2,1)} %bitcast.82), slice={[0:128], [0:28], [0:1152]} | slice | bytes 16515072 | tf_op jit(solution)/shard_map/slice | solution.py:90
  273.1 12.7 %reshape.247 = bf16[3584,1152,1]{1,0,2:T(8,128)(2,1)} reshape(bf16[128,28,1152]{2,1,0:T(8,128)(2,1)} %slice.64) | data formatting | bytes 16515072 | tf_op jit(solution)/shard_map/reshape | solution.py:90
  285.8 5.9 %fusion.2 = f32[4,64,1152]{2,1,0:T(8,128)S(1)} fusion(bf16[4,64,3584]{2,1,0:T(8,128)(2,1)S(1)} %bitcast.90, bf16[3584,1152,1]{1,0,2:T(8,128)(2,1)} %reshape.247, f32[1152]{0:T(1024)S(1)} %copy-done.16, f32[4,1152]{1,0:T(4,128)S(1)} %copy-done.13, f32[4,64]{1,0:T(4,128)S(1)} %broadcast_multiply_fusion.1), kind=kOutput, calls=%fused_computation.8 | convolution fusion | flops 2114813952 | bytes 11296256 | tf_op jit(solution)/shard_map/dot_general | solution.py:99
  292.4 6.6 %slice.72 = bf16[128,28,896]{2,1,0:T(8,128)(2,1)} slice(bf16[128,32,2048]{2,1,0:T(8,128)(2,1)} %bitcast.83), slice={[0:128], [0:28], [1152:2048]} | slice | bytes 12845056 | tf_op jit(solution)/shard_map/slice | solution.py:91
  302.9 10.4 %reshape.252 = bf16[3584,896,1]{1,0,2:T(8,128)(2,1)} reshape(bf16[128,28,896]{2,1,0:T(8,128)(2,1)} %slice.72) | data formatting | bytes 12845056 | tf_op jit(solution)/shard_map/reshape | solution.py:91
  313.3 6.7 %convolution_add_fusion = f32[4,64,3584]{2,1,0:T(8,128)} fusion(bf16[4,64,896]{2,1,0:T(8,128)(2,1)S(1)} %dot_general.36, bf16[3584,896,1]{1,0,2:T(8,128)(2,1)} %reshape.252, f32[4,3584]{1,0:T(4,128)S(1)} %copy-done.9, f32[4,64]{1,0:T(4,128)S(1)} %broadcast_multiply_fusion), kind=kOutput, calls=%fused_computation.2 | convolution fusion | flops 1646002176 | bytes 10609664 | tf_op jit(solution)/shard_map/dot_general | solution.py:132
  320.1 5.1 %copy.70 = f32[256,3584]{0,1:T(8,128)} copy(f32[256,3584]{1,0:T(8,128)} %bitcast.89) | data formatting | bytes 7340032 | tf_op jit(solution)/shard_map/reshape | solution.py:143
  326.7 0.8 copy.71
  327.5 14.4 %all-to-all-start.2 = ((bf16[4,128,56]{2,0,1:T(4,128)(2,1)}), bf16[4,128,56]{2,0,1:T(4,128)(2,1)S(1)}, u32[]{:S(2)}, u32[]{:S(2)}) async-start(bf16[4,128,56]{2,0,1:T(4,128)(2,1)} %copy.71), calls=%async_computation.3 | async-start | bytes 262144 | tf_op jit(solution)/shard_map/all_to_all | solution.py:163
  341.9 0.8 fusion.18
  345.8 2.3 slice.75
  348.1 2.9 slice.77
  351.3 2.5 reshape.236
  353.8 76.5 %all-to-all-done.2 = bf16[4,128,56]{2,0,1:T(4,128)(2,1)S(1)} async-done(((bf16[4,128,56]{2,0,1:T(4,128)(2,1)}), bf16[4,128,56]{2,0,1:T(4,128)(2,1)S(1)}, u32[]{:S(2)}, u32[]{:S(2)}) %all-to-all-start.2) | async-done | bytes 57376 | tf_op jit(solution)/shard_map/all_to_all | solution.py:163
  430.3 2.5 convolution_multiply_fusion.2
  432.9 1.5 convolution_multiply_fusion
  434.4 2.1 multiply_reduce_fusion.2
  (82 shorter events, 13.7 us)
Async XLA Ops:
  7.2 257.9 %all-gather.3.cloned.1.call-start = ((), (), s32[]{:S(2)}) async-start(), calls=%async_computation.5 | async-start | bytes 16908288 | tf_op jit(solution)/shard_map/all_gather | solution.py:89
  11.1 29.6 %all-to-all-start = ((s32[128,4,65]{2,1,0:T(4,128)}), s32[128,4,65]{2,1,0:T(4,128)S(1)}, u32[]{:S(2)}, u32[]{:S(2)}) async-start(s32[128,4,65]{2,1,0:T(4,128)} %broadcast_in_dim.21), calls=%async_computation | async-start | bytes 524288 | tf_op jit(solution)/shard_map/all_to_all | solution.py:77
  169.2 12.1 %copy-start.10 = (bf16[4,1152]{1,0:T(4,128)(2,1)S(1)}, bf16[4,1152]{1,0:T(4,128)(2,1)}, u32[]{:S(2)}) copy-start(bf16[4,1152]{1,0:T(4,128)(2,1)} %param.21) | copy-start | bytes 27652
  169.2 12.7 %copy-start.6 = (bf16[4,3584]{1,0:T(4,128)(2,1)S(1)}, bf16[4,3584]{1,0:T(4,128)(2,1)}, u32[]{:S(2)}) copy-start(bf16[4,3584]{1,0:T(4,128)(2,1)} %param.23) | copy-start | bytes 86020
  169.2 63.7 %all-to-all-start.1 = ((bf16[28,128,256]{2,0,1:T(8,128)(2,1)}), bf16[28,128,256]{2,0,1:T(8,128)(2,1)S(1)}, u32[]{:S(2)}, u32[]{:S(2)}) async-start(bf16[28,128,256]{2,0,1:T(8,128)(2,1)} %broadcast_select_fusion), calls=%async_computation.1 | async-start | bytes 4194304 | tf_op jit(solution)/shard_map/all_to_all | solution.py:95
  181.0 253.3 %reduce-scatter.2.cloned.1.call-start = ((), (), s32[]{:S(2)}) async-start(), calls=%async_computation.4 | async-start | bytes 5505024 | tf_op jit(solution)/shard_map/reduce_scatter | solution.py:142
  232.9 2.1 copy-start.8
  252.9 11.5 %copy-start.11 = (bf16[4,3584]{1,0:T(4,128)(2,1)S(1)}, bf16[4,3584]{1,0:T(4,128)(2,1)}, u32[]{:S(2)}) copy-start(bf16[4,3584]{1,0:T(4,128)(2,1)} %param.20) | copy-start | bytes 86020
  273.1 12.7 %copy-start.2 = (bf16[256,3584]{1,0:T(8,128)(2,1)S(1)}, bf16[256,3584]{1,0:T(8,128)(2,1)}, u32[]{:S(2)}) copy-start(bf16[256,3584]{1,0:T(8,128)(2,1)} %copy.66) | copy-start | bytes 5505028
  273.1 12.7 %copy-start.13 = (f32[4,1152]{1,0:T(4,128)S(1)}, f32[4,1152]{1,0:T(4,128)}, u32[]{:S(2)}) copy-start(f32[4,1152]{1,0:T(4,128)} %convert_element_type.81) | copy-start | bytes 55300
  273.1 12.7 %copy-start.16 = (f32[1152]{0:T(1024)S(1)}, f32[1152]{0:T(1024)}, u32[]{:S(2)}) copy-start(f32[1152]{0:T(1024)} %param.17) | copy-start | bytes 13828
  299.2 0.9 copy-start.3
  299.2 1.0 copy-start.4
  299.2 1.0 copy-start.5
  301.4 1.2 copy-start.15
  302.9 10.5 %copy-start.9 = (f32[4,3584]{1,0:T(4,128)S(1)}, f32[4,3584]{1,0:T(4,128)}, u32[]{:S(2)}) copy-start(f32[4,3584]{1,0:T(4,128)} %convert_element_type.88) | copy-start | bytes 172036
  325.2 0.7 copy-start.12
  325.2 1.1 copy-start.7
  327.5 102.8 %all-to-all-start.2 = ((bf16[4,128,56]{2,0,1:T(4,128)(2,1)}), bf16[4,128,56]{2,0,1:T(4,128)(2,1)S(1)}, u32[]{:S(2)}, u32[]{:S(2)}) async-start(bf16[4,128,56]{2,0,1:T(4,128)(2,1)} %copy.71), calls=%async_computation.3 | async-start | bytes 262144 | tf_op jit(solution)/shard_map/all_to_all | solution.py:163
  351.3 83.1 %copy-start = (bf16[3584,256]{1,0:T(8,128)(2,1)S(1)}, bf16[3584,256]{1,0:T(8,128)(2,1)}, u32[]{:S(2)}) copy-start(bf16[3584,256]{1,0:T(8,128)(2,1)} %all_to_all.31) | copy-start | bytes 5505028
  432.9 3.6 copy-start.14
  434.4 2.1 copy-start.1
Sparse Core Ops, SparseCore 0:
  10.4 236.2 all-gather.2
  325.3 87.9 reduce-scatter.1

commit v2 on v1

--- a/solution.py
+++ b/solution.py
@@ -68,17 +68,17 @@
     mp_size = lax.axis_size("mp")
     heads_here = HQ // mp_size
     kv_here = HK // mp_size
-    population = members * lax.axis_size("member")
+    member_count = lax.axis_size("member")
+    population = members * member_count
+    feature_rows = qkv_weight.shape[0]
+    qkv_cols = qkv_weight.shape[1]
+    out_cols = out_weight.shape[1]
     contract_rows = (((0,), (0,)), ((), ()))
-    contract_cols = (((1,), (1,)), ((), ()))
-    member_count = lax.axis_size("member")
     packed_ids = jnp.concatenate([token_ids, fit_ranks[:, None]], axis=1)
     spread_ids = jnp.broadcast_to(packed_ids[None], (member_count,) + packed_ids.shape)
     every_ids = lax.all_to_all(spread_ids, "member", split_axis=0, concat_axis=0, tiled=True)
     all_ids = every_ids[:, :, :length].reshape(population, length)
     all_ranks = every_ids[:, :, length].reshape(population)
-    feature_rows = qkv_weight.shape[0]
-    qkv_cols = qkv_weight.shape[1]
     stacked = jnp.concatenate(
         [
             jnp.concatenate([qkv_weight, out_weight], axis=1),
@@ -87,23 +87,39 @@
         axis=0,
     )
     gathered = lax.all_gather(stacked, "member", axis=0)
-    full_qkv = gathered[:, :feature_rows, :qkv_cols].reshape(-1, qkv_cols)
-    full_out = gathered[:, :feature_rows, qkv_cols:].reshape(-1, out_weight.shape[1])
+    block_qkv = gathered[:, :feature_rows, :qkv_cols]
+    block_out = gathered[:, :feature_rows, qkv_cols:]
     right_cols = gathered[:, feature_rows:, :qkv_cols].reshape(population, qkv_cols)
-    left_cols = gathered[:, feature_rows:, qkv_cols:].reshape(population, out_left.shape[1])
+    left_cols = gathered[:, feature_rows:, qkv_cols:].reshape(population, out_cols)
     picked = jnp.take(embed_table, all_ids.reshape(-1), axis=1)
-    embedded = lax.all_to_all(picked, "member", split_axis=1, concat_axis=0, tiled=True)
+    token_block = row_count
+    factor_width = 2 * feature_rows * members
+    factors = jnp.concatenate(
+        [
+            qkv_left.reshape(members, member_count, feature_rows),
+            out_right.reshape(members, member_count, feature_rows),
+        ],
+        axis=2,
+    )
+    factors = factors.transpose(1, 0, 2).reshape(member_count, factor_width)
+    factors = jnp.pad(factors, ((0, 0), (0, token_block - factor_width))).reshape(1, -1)
+    combined = jnp.concatenate([picked, factors], axis=0)
+    arrived = lax.all_to_all(combined, "member", split_axis=1, concat_axis=0, tiled=True)
+    arrived = arrived.reshape(member_count, feature_rows + 1, token_block)
+    embedded = arrived[:, :feature_rows, :]
+    factor_cols = arrived[:, feature_rows, :factor_width].reshape(population, 2 * feature_rows)
+    left_rows = factor_cols[:, :feature_rows]
+    right_rows = factor_cols[:, feature_rows:]
     features = embedded.astype(jnp.float32)
-    inverse_rms = lax.rsqrt(jnp.mean(features * features, axis=0, keepdims=True) + EPSILON)
-    normed = (features * inverse_rms * norm_gain[:, None]).astype(jnp.bfloat16)
-    base_proj = lax.dot_general(
-        normed,
-        full_qkv,
-        contract_rows,
-        preferred_element_type=jnp.float32,
-    )
-    normed_members = normed.reshape(normed.shape[0], members, length)
-    coef_in = jnp.einsum("dms,md->ms", normed_members, qkv_left, preferred_element_type=jnp.float32)
+    inverse_rms = lax.rsqrt(jnp.mean(features * features, axis=(0, 1), keepdims=True) + EPSILON)
+    gain = norm_gain.reshape(member_count, feature_rows, 1)
+    normed = (features * inverse_rms * gain).astype(jnp.bfloat16)
+    base_proj = jnp.einsum("abt,abn->tn", normed, block_qkv, preferred_element_type=jnp.float32)
+    normed_members = normed.reshape(member_count, feature_rows, members, length)
+    left_blocks = qkv_left.reshape(members, member_count, feature_rows)
+    coef_in = jnp.einsum(
+        "abms,mab->ms", normed_members, left_blocks, preferred_element_type=jnp.float32
+    )
     projected = (
         base_proj.reshape(members, length, -1)
         + SIGMA * coef_in[:, :, None] * qkv_right.astype(jnp.float32)[:, None, :]
@@ -128,41 +144,33 @@
     context = attend(query_heads, key_heads, value_heads, kv_here)
     coef_out = jnp.einsum("msq,mq->ms", context, out_left, preferred_element_type=jnp.float32)
     flat_context = context.reshape(row_count, query_width)
-    share_rows = row_count // mp_size
-    partial_out = lax.dot_general(
-        flat_context,
-        full_out,
-        contract_cols,
-        preferred_element_type=jnp.float32,
-    )
-    head_term = (
-        partial_out.reshape(members, length, -1)
-        + SIGMA * coef_out[:, :, None] * out_right.astype(jnp.float32)[:, None, :]
-    )
-    summed = lax.psum_scatter(
-        head_term.reshape(row_count, -1), "mp", scatter_dimension=0, tiled=True
-    )
+    partial_out = jnp.einsum(
+        "tc,abc->abt", flat_context, block_out, preferred_element_type=jnp.float32
+    )
+    right_blocks = out_right.reshape(members, member_count, feature_rows).astype(jnp.float32)
+    head_term = partial_out.reshape(member_count, feature_rows, members, length) + SIGMA * (
+        right_blocks.transpose(1, 2, 0)[:, :, :, None] * coef_out[None, None, :, :]
+    )
+    share = members // mp_size
+    head_term = head_term.reshape(member_count, feature_rows, mp_size, share * length)
     mp_index = lax.axis_index("mp")
-    own_embed = lax.dynamic_slice_in_dim(embedded, mp_index * share_rows, share_rows, 1)
-    residual = own_embed.T.astype(jnp.float32) + summed
-    inverse_out = lax.rsqrt(jnp.mean(residual * residual, axis=1, keepdims=True) + EPSILON)
-    value_rows = jnp.sum(residual * inverse_out * value_weight[None, :], axis=1).reshape(
-        members // mp_size, length
-    )
+    own_term = lax.dynamic_index_in_dim(head_term, mp_index, axis=2, keepdims=False)
+    sent_term = lax.dynamic_index_in_dim(head_term, 1 - mp_index, axis=2, keepdims=False)
+    got_term = lax.ppermute(sent_term.astype(jnp.bfloat16), "mp", perm=[(0, 1), (1, 0)])
+    own_embed = lax.dynamic_index_in_dim(
+        features.reshape(member_count, feature_rows, mp_size, share * length),
+        mp_index,
+        axis=2,
+        keepdims=False,
+    )
+    residual = own_embed + own_term + got_term.astype(jnp.float32)
+    inverse_out = lax.rsqrt(jnp.mean(residual * residual, axis=(0, 1), keepdims=True) + EPSILON)
+    value_gain = value_weight.reshape(member_count, feature_rows, 1)
+    value_rows = jnp.sum(residual * inverse_out * value_gain, axis=(0, 1)).reshape(share, length)
     rank_values = all_ranks.astype(jnp.float32)
     center = jnp.sum(rank_values) / population
     spread = jnp.sum(rank_values * rank_values) / population - center * center
     fitness = (rank_values - center) * lax.rsqrt(spread + EPSILON)
-    factor_rows = jnp.concatenate(
-        [
-            qkv_left.reshape(members, member_count, feature_rows),
-            out_right.reshape(members, member_count, feature_rows),
-        ],
-        axis=2,
-    )
-    factor_cols = lax.all_to_all(factor_rows, "member", split_axis=1, concat_axis=0, tiled=True)
-    left_rows = factor_cols[:, 0, :feature_rows]
-    right_rows = factor_cols[:, 0, feature_rows:]
     weighted_in = left_rows.astype(jnp.float32) * fitness[:, None]
     qkv_grad = lax.dot_general(
         weighted_in,

time: 447 us -> 344 us (0.77)
  the two profiles are of different devices: /device:TPU:1 before, /device:TPU:37 now
where the time goes in v2:
time: 344 us; the launch traced here: 343 us
  local copies, waits for them, and re-layouts  177 us (51%)
  waiting for transfers between devices  84.8 us (25%)
  starting transfers between devices  28.1 us (8%)
  matrix products  20.4 us (6%)
  between operations  17.1 us (5%)
  other arithmetic  16.1 us (5%)
    gather x2, local copies, waits for them, and re-layouts, on_device(): picked = jnp.take(embed_table, all_ids.reshape(-1), axis=1)  126 us
    all_to_all x1, waiting for transfers between devices, on_device(): lax.all_to_all(combined, 'member', split_axis=1, concat_axis=0, tiled=True)  44 us
    ppermute x1, waiting for transfers between devices, on_device(): lax.ppermute(sent_term.astype(jnp.bfloat16), 'mp', perm=[(0, 1), (1, 0)])  32.2 us
    unnamed x26, local copies, waits for them, and re-layouts  19.5 us
    all_to_all x1, starting transfers between devices, on_device(): lax.all_to_all(spread_ids, 'member', split_axis=0, concat_axis=0, tiled=T...  12.7 us
    all_to_all x1, starting transfers between devices, on_device(): lax.all_to_all(combined, 'member', split_axis=1, concat_axis=0, tiled=True)  12.3 us
    dot_general x1, matrix products, on_device(): jnp.einsum('abt,abn->tn', normed, block_qkv, preferred_element_type=jnp.f...  9.63 us
    all_gather x1, waiting for transfers between devices, on_device(): gathered = lax.all_gather(stacked, 'member', axis=0)  8.62 us
  transfers between devices with their start and end apart: 4, of which 3 were waited for; matrix products, arithmetic and copies ran while one was open for 48% of the time, Pallas kernels for 0%

profile of v2, /device:TPU:37, one launch (start us, length us, event | category | flops | bytes accessed | tf_op | source)
XLA Modules:
  0.0 343.3 jit_solution(39341350262511848)
XLA Ops:
  7.2 1.6 maximum_maximum_fusion
  11.1 12.7 %all-to-all-start = ((s32[128,4,65]{2,1,0:T(4,128)}), s32[128,4,65]{2,1,0:T(4,128)S(1)}, u32[]{:S(2)}, u32[]{:S(2)}) async-start(s32[128,4,65]{2,1,0:T(4,128)} %broadcast_in_dim.21), calls=%async_computation | async-start | bytes 524288 | tf_op jit(solution)/shard_map/all_to_all | solution.py:79
  23.8 15.7 %copy.63 = bf16[28,76032]{0,1:T(8,128)(2,1)} copy(bf16[28,76032]{1,0:T(8,128)(2,1)} %param.14) | data formatting | bytes 8515584 | tf_op args[2]
  41.2 118.6 %gather_fusion = bf16[32768,28]{1,0:T(8,128)(2,1)} fusion(bf16[28,76032]{0,1:T(8,128)(2,1)} %copy.63, s32[32768]{0:T(1024)S(1)} %broadcast_clamp_fusion), kind=kCustom, calls=%fused_computation | custom fusion | bytes 3801088 | tf_op jit(solution)/shard_map/jit(_take)/gather | solution.py:94
  159.8 7.6 %copy.64 = bf16[28,128,256]{2,0,1:T(8,128)(2,1)S(1)} copy(bf16[28,128,256]{0,2,1:T(8,128)(2,1)} %bitcast.118) | data formatting | bytes 3670016 | tf_op jit(solution)/shard_map/jit(_take)/gather | solution.py:94
  167.8 1.8 pad_maximum_fusion
  169.7 12.3 %all-to-all-start.1 = ((bf16[29,128,256]{2,0,1:T(8,128)(2,1)}), bf16[29,128,256]{2,0,1:T(8,128)(2,1)}, u32[]{:S(2)}, u32[]{:S(2)}) async-start(bf16[29,128,256]{2,0,1:T(8,128)(2,1)} %pad_maximum_fusion), calls=%async_computation.1 | async-start | bytes 4194304 | tf_op jit(solution)/shard_map/all_to_all | solution.py:107
  183.3 0.8 fusion.18
  186.7 44.0 %all-to-all-done.1 = bf16[29,128,256]{2,0,1:T(8,128)(2,1)} async-done(((bf16[29,128,256]{2,0,1:T(8,128)(2,1)}), bf16[29,128,256]{2,0,1:T(8,128)(2,1)}, u32[]{:S(2)}, u32[]{:S(2)}) %all-to-all-start.1) | async-done | bytes 1900576 | tf_op jit(solution)/shard_map/all_to_all | solution.py:107
  230.7 3.8 %copy.68 = bf16[29,128,256]{1,2,0:T(8,128)(2,1)S(1)} copy(bf16[29,128,256]{2,0,1:T(8,128)(2,1)} %all-to-all-done.1) | data formatting | bytes 3801088 | tf_op jit(solution)/shard_map/all_to_all | solution.py:107
  235.7 1.2 copy-done.3
  237.4 8.6 %all-gather.3.cloned.1.call-done = bf16[4096,2048]{1,0:T(8,128)(2,1)} async-done(((bf16[32,2048]{1,0:T(8,128)(2,1)}), bf16[4096,2048]{1,0:T(8,128)(2,1)}) %all-gather.3.cloned.1.call-update) | async-done | bytes 16777232 | tf_op jit(solution)/shard_map/all_gather | solution.py:89
  246.1 8.0 %slice.74 = bf16[128,28,1152]{2,1,0:T(8,128)(2,1)} slice(bf16[128,32,2048]{2,1,0:T(8,128)(2,1)} %bitcast.112), slice={[0:128], [0:28], [0:1152]} | slice | bytes 16515072 | tf_op jit(solution)/shard_map/slice | solution.py:90
  254.1 9.6 %fusion = f32[256,1152,1]{1,0,2:T(8,128)S(1)} fusion(bf16[128,28,256]{0,2,1:T(8,128)(2,1)} %copy-done.3, bf16[128,28,1152]{2,1,0:T(8,128)(2,1)} %slice.74), kind=kOutput, calls=%fused_computation.1 | convolution fusion | flops 2113929216 | bytes 11272192 | tf_op jit(solution)/shard_map/abt,abn->tn/dot_general | solution.py:117
  264.0 1.1 slice.79
  265.3 1.3 reshape.215
  267.5 1.5 fusion.37
  269.1 1.2 fusion.7
  270.7 1.3 dot_general.30
  272.6 3.7 %slice.73 = bf16[128,28,896]{2,1,0:T(8,128)(2,1)S(1)} slice(bf16[128,32,2048]{2,1,0:T(8,128)(2,1)} %bitcast.113), slice={[0:128], [0:28], [1152:2048]} | slice | bytes 12845056 | tf_op jit(solution)/shard_map/slice | solution.py:91
  276.6 4.4 %multiply_add_fusion = f32[128,28,4,64]{0,3,2,1:T(8,128)S(1)} fusion(bf16[4,64,896,1]{2,1,0,3:T(8,128)(2,1)S(1)} %reshape.236, bf16[128,28,896]{2,1,0:T(8,128)(2,1)S(1)} %slice.73, f32[4,64]{1,0:T(4,128)S(1)} %bitcast.131, f32[128,28,4]{0,2,1:T(4,128)S(1)} %copy.76), kind=kOutput, calls=%fused_computation.5 | convolution fusion | flops 1646919680 | bytes 10609664 | tf_op jit(solution)/shard_map/tc,abc->abt/dot_general | solution.py:147
  281.0 1.8 copy-done.1
  282.8 1.1 fusion.10
  283.9 3.1 collective-permute-start
  287.7 2.3 slice_convert_fusion
  289.9 2.3 slice.85
  292.2 2.0 slice.87
  295.0 1.4 convolution_multiply_fusion.2
  296.3 1.5 convolution_multiply_fusion
  297.8 32.2 %collective-permute-done = bf16[128,28,128]{0,2,1:T(8,128)(2,1)} collective-permute-done((bf16[128,28,128]{0,2,1:T(8,128)(2,1)}, bf16[128,28,128]{0,2,1:T(8,128)(2,1)}, u32[]{:S(2)}, u32[]{:S(2)}) %collective-permute-start) | collective-permute-done | bytes 917536 | tf_op jit(solution)/shard_map/ppermute | solution.py:159
  330.0 2.9 multiply_reduce_fusion.2
  333.4 2.3 multiply_reduce_fusion.1
  (78 shorter events, 12.3 us)
Async XLA Ops:
  7.2 238.9 %all-gather.3.cloned.1.call-start = ((), (), s32[]{:S(2)}) async-start(), calls=%async_computation.2 | async-start | bytes 16908288 | tf_op jit(solution)/shard_map/all_gather | solution.py:89
  11.1 29.5 %all-to-all-start = ((s32[128,4,65]{2,1,0:T(4,128)}), s32[128,4,65]{2,1,0:T(4,128)S(1)}, u32[]{:S(2)}, u32[]{:S(2)}) async-start(s32[128,4,65]{2,1,0:T(4,128)} %broadcast_in_dim.21), calls=%async_computation | async-start | bytes 524288 | tf_op jit(solution)/shard_map/all_to_all | solution.py:79
  23.8 15.8 %copy-start.7 = (bf16[4,3584]{1,0:T(4,128)(2,1)S(1)}, bf16[4,3584]{1,0:T(4,128)(2,1)}, u32[]{:S(2)}) copy-start(bf16[4,3584]{1,0:T(4,128)(2,1)} %param.23) | copy-start | bytes 86020
  23.8 16.2 %copy-start.5 = (bf16[4,3584]{1,0:T(4,128)(2,1)S(1)}, bf16[4,3584]{1,0:T(4,128)(2,1)}, u32[]{:S(2)}) copy-start(bf16[4,3584]{1,0:T(4,128)(2,1)} %param.20) | copy-start | bytes 86020
  169.7 12.6 %copy-start.6 = (bf16[4,1152]{1,0:T(4,128)(2,1)S(1)}, bf16[4,1152]{1,0:T(4,128)(2,1)}, u32[]{:S(2)}) copy-start(bf16[4,1152]{1,0:T(4,128)(2,1)} %param.21) | copy-start | bytes 27652
  169.7 12.7 %copy-start.8 = (f32[3584]{0:T(1024)S(1)}, f32[3584]{0:T(1024)}, u32[]{:S(2)}) copy-start(f32[3584]{0:T(1024)} %param.15) | copy-start | bytes 43012
  169.7 13.2 %copy-start.9 = (f32[3584]{0:T(1024)S(1)}, f32[3584]{0:T(1024)}, u32[]{:S(2)}) copy-start(f32[3584]{0:T(1024)} %param.19) | copy-start | bytes 43012
  169.7 61.0 %all-to-all-start.1 = ((bf16[29,128,256]{2,0,1:T(8,128)(2,1)}), bf16[29,128,256]{2,0,1:T(8,128)(2,1)}, u32[]{:S(2)}, u32[]{:S(2)}) async-start(bf16[29,128,256]{2,0,1:T(8,128)(2,1)} %pad_maximum_fusion), calls=%async_computation.1 | async-start | bytes 4194304 | tf_op jit(solution)/shard_map/all_to_all | solution.py:107
  235.7 1.2 copy-start.3
  254.1 9.6 %copy-start.10 = (f32[1152]{0:T(1024)S(1)}, f32[1152]{0:T(1024)}, u32[]{:S(2)}) copy-start(f32[1152]{0:T(1024)} %param.17) | copy-start | bytes 13828
  264.0 1.3 copy-start.2
  272.5 3.8 %copy-start.4 = (bf16[4,64,896]{2,1,0:T(8,128)(2,1)S(1)}, bf16[4,64,896]{2,1,0:T(8,128)(2,1)}, u32[]{:S(2)}) copy-start(bf16[4,64,896]{2,1,0:T(8,128)(2,1)} %dot_general.30) | copy-start | bytes 1376260
  272.6 3.8 %copy-start.11 = (bf16[4,896]{1,0:T(4,128)(2,1)S(1)}, bf16[4,896]{1,0:T(4,128)(2,1)}, u32[]{:S(2)}) copy-start(bf16[4,896]{1,0:T(4,128)(2,1)} %param.22) | copy-start | bytes 21508
  281.0 1.8 copy-start.1
  283.9 46.1 %collective-permute-start = (bf16[128,28,128]{0,2,1:T(8,128)(2,1)}, bf16[128,28,128]{0,2,1:T(8,128)(2,1)}, u32[]{:S(2)}, u32[]{:S(2)}) collective-permute-start(bf16[128,28,128]{0,2,1:T(8,128)(2,1)} %fusion.10), channel_id=1, source_target_pairs={{0,1},{1,0},{2,3},{3,2},{4,5},{5,4},{6,7},{7,6},{8,9},{9,8},{10,11... | collective-permute-start | bytes 2752520 | tf_op jit(solution)/shard_map/ppermute | solution.py:159
  330.0 3.4 copy-start
Sparse Core Ops, SparseCore 0:
  10.4 235.6 all-gather.2

commit v3 on v2

--- a/solution.py
+++ b/solution.py
@@ -14,6 +14,7 @@
 EPSILON = 1e-06
 THETA = 1000000.0
 MASKED = -1e30
+MEMBER = ("y", "zl", "x", "c")
 
 
 def rope_tables(length, head_size):
@@ -68,7 +69,7 @@
     mp_size = lax.axis_size("mp")
     heads_here = HQ // mp_size
     kv_here = HK // mp_size
-    member_count = lax.axis_size("member")
+    member_count = lax.axis_size(MEMBER)
     population = members * member_count
     feature_rows = qkv_weight.shape[0]
     qkv_cols = qkv_weight.shape[1]
@@ -76,7 +77,7 @@
     contract_rows = (((0,), (0,)), ((), ()))
     packed_ids = jnp.concatenate([token_ids, fit_ranks[:, None]], axis=1)
     spread_ids = jnp.broadcast_to(packed_ids[None], (member_count,) + packed_ids.shape)
-    every_ids = lax.all_to_all(spread_ids, "member", split_axis=0, concat_axis=0, tiled=True)
+    every_ids = lax.all_to_all(spread_ids, MEMBER, split_axis=0, concat_axis=0, tiled=True)
     all_ids = every_ids[:, :, :length].reshape(population, length)
     all_ranks = every_ids[:, :, length].reshape(population)
     stacked = jnp.concatenate(
@@ -86,7 +87,11 @@
         ],
         axis=0,
     )
-    gathered = lax.all_gather(stacked, "member", axis=0)
+    gathered = lax.all_gather(stacked, "x", axis=0)
+    gathered = lax.all_gather(gathered, "zl", axis=0)
+    gathered = lax.all_gather(gathered, "y", axis=0)
+    gathered = lax.all_gather(gathered, "c", axis=3)
+    gathered = gathered.reshape((member_count,) + stacked.shape)
     block_qkv = gathered[:, :feature_rows, :qkv_cols]
     block_out = gathered[:, :feature_rows, qkv_cols:]
     right_cols = gathered[:, feature_rows:, :qkv_cols].reshape(population, qkv_cols)
@@ -104,7 +109,7 @@
     factors = factors.transpose(1, 0, 2).reshape(member_count, factor_width)
     factors = jnp.pad(factors, ((0, 0), (0, token_block - factor_width))).reshape(1, -1)
     combined = jnp.concatenate([picked, factors], axis=0)
-    arrived = lax.all_to_all(combined, "member", split_axis=1, concat_axis=0, tiled=True)
+    arrived = lax.all_to_all(combined, MEMBER, split_axis=1, concat_axis=0, tiled=True)
     arrived = arrived.reshape(member_count, feature_rows + 1, token_block)
     embedded = arrived[:, :feature_rows, :]
     factor_cols = arrived[:, feature_rows, :factor_width].reshape(population, 2 * feature_rows)
@@ -191,24 +196,29 @@
 
 
 def solution(mesh):
+    member_size, mp_size = mesh.devices.shape
+    chips = member_size // (2 * 4 * 4)
+    split_mesh = jax.sharding.Mesh(
+        mesh.devices.reshape(chips, 4, 4, 2, mp_size), ("y", "zl", "x", "c", "mp")
+    )
     placed = (
-        P("member", None),
-        P("member"),
-        P("member", None),
+        P(MEMBER, None),
+        P(MEMBER),
+        P(MEMBER, None),
         P(),
-        P("member", "mp"),
+        P(MEMBER, "mp"),
         P("mp"),
-        P("member", "mp"),
+        P(MEMBER, "mp"),
         P(),
-        P("member", None),
-        P("member", "mp"),
-        P("member", "mp"),
-        P("member", None),
+        P(MEMBER, None),
+        P(MEMBER, "mp"),
+        P(MEMBER, "mp"),
+        P(MEMBER, None),
     )
     return jax.shard_map(
         on_device,
-        mesh=mesh,
+        mesh=split_mesh,
         in_specs=placed,
-        out_specs=(P(("member", "mp"), None), P("member", "mp"), P("member", "mp")),
+        out_specs=(P(MEMBER + ("mp",), None), P(MEMBER, "mp"), P(MEMBER, "mp")),
         check_vma=False,
     )

time: 344 us -> 491 us (1.43)
  the two profiles are of different devices: /device:TPU:37 before, /device:TPU:1 now
where the time goes in v3:
time: 491 us; the launch traced here: 490 us
  waiting for transfers between devices  221 us (45%)
  local copies, waits for them, and re-layouts  177 us (36%)
  starting transfers between devices  26.9 us (5%)
  matrix products  20.4 us (4%)
  between operations  16.8 us (3%)
  other arithmetic  14.7 us (3%)
  blocking collectives  12.8 us (3%)
    gather x2, local copies, waits for them, and re-layouts, on_device(): picked = jnp.take(embed_table, all_ids.reshape(-1), axis=1)  126 us
    all_gather x1, waiting for transfers between devices, on_device(): gathered = lax.all_gather(gathered, 'y', axis=0)  87.3 us
    all_gather x1, waiting for transfers between devices, on_device(): gathered = lax.all_gather(gathered, 'zl', axis=0)  54.5 us
    all_to_all x1, waiting for transfers between devices, on_device(): lax.all_to_all(combined, MEMBER, split_axis=1, concat_axis=0, tiled=True)  46.8 us
    ppermute x1, waiting for transfers between devices, on_device(): lax.ppermute(sent_term.astype(jnp.bfloat16), 'mp', perm=[(0, 1), (1, 0)])  32.2 us
    unnamed x30, local copies, waits for them, and re-layouts  20.8 us
    all_gather x1, blocking collectives, on_device(): gathered = lax.all_gather(stacked, 'x', axis=0)  12.8 us
    all_to_all x1, starting transfers between devices, on_device(): lax.all_to_all(combined, MEMBER, split_axis=1, concat_axis=0, tiled=True)  12.5 us
  transfers between devices with their start and end apart: 6, of which 4 were waited for; matrix products, arithmetic and copies ran while one was open for 34% of the time, Pallas kernels for 0%

profile of v3, /device:TPU:1, one launch (start us, length us, event | category | flops | bytes accessed | tf_op | source)
XLA Modules:
  0.0 489.7 jit_solution(9971236045777299969)
XLA Ops:
  8.2 12.8 %all-gather = bf16[128,2048]{1,0:T(8,128)(2,1)} all-gather(bf16[32,2048]{1,0:T(8,128)(2,1)S(1)} %maximum_maximum_fusion), channel_id=2, replica_groups=mesh['y'=4,'zl'=4,'x'=4,'c'=2,'mp'=2] {'x'}, dimensions={0}, use_global_device_ids=true | all-gather | bytes 655360 | tf_op jit(solution)/shard_map/all_gather | solution.py:90
  21.0 54.5 %all-gather.8.cloned.1.call-done = bf16[16,32,2048]{2,1,0:T(8,128)(2,1)} async-done(((bf16[4,32,2048]{2,1,0:T(8,128)(2,1)}), bf16[16,32,2048]{2,1,0:T(8,128)(2,1)}) %all-gather.8.cloned.1.call-update) | async-done | bytes 2097168 | tf_op jit(solution)/shard_map/all_gather | solution.py:91
  75.6 87.3 %all-gather.10.cloned.1.call-done = bf16[16,4,32,2048]{3,2,1,0:T(8,128)(2,1)} async-done(((bf16[4,4,32,2048]{3,2,1,0:T(8,128)(2,1)}), bf16[16,4,32,2048]{3,2,1,0:T(8,128)(2,1)}) %all-gather.10.cloned.1.call-update) | async-done | bytes 8388624 | tf_op jit(solution)/shard_map/all_gather | solution.py:92
  164.6 11.5 %all-to-all-start = ((s32[128,4,65]{2,1,0:T(4,128)}), s32[128,4,65]{2,1,0:T(4,128)S(1)}, u32[]{:S(2)}, u32[]{:S(2)}) async-start(s32[128,4,65]{2,1,0:T(4,128)} %broadcast_in_dim.21), calls=%async_computation | async-start | bytes 524288 | tf_op jit(solution)/shard_map/all_to_all | solution.py:80
  176.1 16.3 %copy.63 = bf16[28,76032]{0,1:T(8,128)(2,1)} copy(bf16[28,76032]{1,0:T(8,128)(2,1)} %param.14) | data formatting | bytes 8515584 | tf_op args[2]
  194.1 118.4 %gather_fusion = bf16[32768,28]{1,0:T(8,128)(2,1)} fusion(bf16[28,76032]{0,1:T(8,128)(2,1)} %copy.63, s32[32768]{0:T(1024)S(1)} %broadcast_clamp_fusion), kind=kCustom, calls=%fused_computation | custom fusion | bytes 3801088 | tf_op jit(solution)/shard_map/jit(_take)/gather | solution.py:99
  312.5 7.5 %copy.64 = bf16[28,128,256]{2,0,1:T(8,128)(2,1)S(1)} copy(bf16[28,128,256]{0,2,1:T(8,128)(2,1)} %bitcast.121) | data formatting | bytes 3670016 | tf_op jit(solution)/shard_map/jit(_take)/gather | solution.py:99
  320.5 1.8 pad_maximum_fusion
  322.4 12.5 %all-to-all-start.1 = ((bf16[29,128,256]{2,0,1:T(8,128)(2,1)}), bf16[29,128,256]{2,0,1:T(8,128)(2,1)}, u32[]{:S(2)}, u32[]{:S(2)}) async-start(bf16[29,128,256]{2,0,1:T(8,128)(2,1)} %pad_maximum_fusion), calls=%async_computation.1 | async-start | bytes 4194304 | tf_op jit(solution)/shard_map/all_to_all | solution.py:112
  339.6 46.8 %all-to-all-done.1 = bf16[29,128,256]{2,0,1:T(8,128)(2,1)} async-done(((bf16[29,128,256]{2,0,1:T(8,128)(2,1)}), bf16[29,128,256]{2,0,1:T(8,128)(2,1)}, u32[]{:S(2)}, u32[]{:S(2)}) %all-to-all-start.1) | async-done | bytes 1900576 | tf_op jit(solution)/shard_map/all_to_all | solution.py:112
  386.4 3.8 copy.68
  391.3 1.2 copy-done.3
  393.1 8.1 %slice.74 = bf16[128,28,1152]{2,1,0:T(8,128)(2,1)} slice(bf16[128,32,2048]{2,1,0:T(8,128)(2,1)} %bitcast.115), slice={[0:128], [0:28], [0:1152]} | slice | bytes 16515072 | tf_op jit(solution)/shard_map/slice | solution.py:95
  401.2 9.6 %fusion = f32[256,1152,1]{1,0,2:T(8,128)S(1)} fusion(bf16[128,28,256]{0,2,1:T(8,128)(2,1)} %copy-done.3, bf16[128,28,1152]{2,1,0:T(8,128)(2,1)} %slice.74), kind=kOutput, calls=%fused_computation.1 | convolution fusion | flops 2113929216 | bytes 11272192 | tf_op jit(solution)/shard_map/abt,abn->tn/dot_general | solution.py:122
  411.1 1.1 slice.79
  412.4 1.3 reshape.219
  414.6 1.5 fusion.37
  416.2 1.2 fusion.7
  417.8 1.3 dot_general.30
  419.7 3.7 slice.73
  423.7 4.4 multiply_add_fusion
  428.1 1.8 copy-done.1
  429.9 1.1 fusion.10
  431.0 2.8 collective-permute-start
  434.5 2.2 slice_convert_fusion
  436.7 2.3 slice.85
  439.0 2.0 slice.87
  441.8 1.4 convolution_multiply_fusion.2
  443.1 1.5 convolution_multiply_fusion
  444.6 32.2 %collective-permute-done = bf16[128,28,128]{0,2,1:T(8,128)(2,1)} collective-permute-done((bf16[128,28,128]{0,2,1:T(8,128)(2,1)}, bf16[128,28,128]{0,2,1:T(8,128)(2,1)}, u32[]{:S(2)}, u32[]{:S(2)}) %collective-permute-start) | collective-permute-done | bytes 917536 | tf_op jit(solution)/shard_map/ppermute | solution.py:164
  476.8 2.9 multiply_reduce_fusion.2
  480.2 2.3 multiply_reduce_fusion.1
  (89 shorter events, 13.6 us)
Async XLA Ops:
  7.2 68.4 %all-gather.8.cloned.1.call-start = ((), (), s32[]{:S(2)}) async-start(), calls=%async_computation.2 | async-start | bytes 2621440 | tf_op jit(solution)/shard_map/all_gather | solution.py:91
  21.0 142.0 %all-gather.10.cloned.1.call-start = ((), (), s32[]{:S(2)}) async-start(), calls=%async_computation.3 | async-start | bytes 10485760 | tf_op jit(solution)/shard_map/all_gather | solution.py:92
  75.6 317.5 %all-gather.12.cloned.1.call-start = ((), (), s32[]{:S(2)}) async-start(), calls=%async_computation.4 | async-start | bytes 25165824 | tf_op jit(solution)/shard_map/all_gather | solution.py:93
  163.0 0.7 copy-start.13
  163.0 0.7 copy-start.12
  164.6 29.0 %all-to-all-start = ((s32[128,4,65]{2,1,0:T(4,128)}), s32[128,4,65]{2,1,0:T(4,128)S(1)}, u32[]{:S(2)}, u32[]{:S(2)}) async-start(s32[128,4,65]{2,1,0:T(4,128)} %broadcast_in_dim.21), calls=%async_computation | async-start | bytes 524288 | tf_op jit(solution)/shard_map/all_to_all | solution.py:80
  176.1 16.3 %copy-start.7 = (bf16[4,3584]{1,0:T(4,128)(2,1)S(1)}, bf16[4,3584]{1,0:T(4,128)(2,1)}, u32[]{:S(2)}) copy-start(bf16[4,3584]{1,0:T(4,128)(2,1)} %param.23) | copy-start | bytes 86020
  176.1 16.8 %copy-start.5 = (bf16[4,3584]{1,0:T(4,128)(2,1)S(1)}, bf16[4,3584]{1,0:T(4,128)(2,1)}, u32[]{:S(2)}) copy-start(bf16[4,3584]{1,0:T(4,128)(2,1)} %param.20) | copy-start | bytes 86020
  322.4 12.8 %copy-start.6 = (bf16[4,1152]{1,0:T(4,128)(2,1)S(1)}, bf16[4,1152]{1,0:T(4,128)(2,1)}, u32[]{:S(2)}) copy-start(bf16[4,1152]{1,0:T(4,128)(2,1)} %param.21) | copy-start | bytes 27652
  322.4 12.8 %copy-start.8 = (f32[3584]{0:T(1024)S(1)}, f32[3584]{0:T(1024)}, u32[]{:S(2)}) copy-start(f32[3584]{0:T(1024)} %param.15) | copy-start | bytes 43012
  322.4 13.3 %copy-start.9 = (f32[3584]{0:T(1024)S(1)}, f32[3584]{0:T(1024)}, u32[]{:S(2)}) copy-start(f32[3584]{0:T(1024)} %param.19) | copy-start | bytes 43012
  322.4 64.0 %all-to-all-start.1 = ((bf16[29,128,256]{2,0,1:T(8,128)(2,1)}), bf16[29,128,256]{2,0,1:T(8,128)(2,1)}, u32[]{:S(2)}, u32[]{:S(2)}) async-start(bf16[29,128,256]{2,0,1:T(8,128)(2,1)} %pad_maximum_fusion), calls=%async_computation.1 | async-start | bytes 4194304 | tf_op jit(solution)/shard_map/all_to_all | solution.py:112
  391.3 1.2 copy-start.3
  401.2 9.7 %copy-start.10 = (f32[1152]{0:T(1024)S(1)}, f32[1152]{0:T(1024)}, u32[]{:S(2)}) copy-start(f32[1152]{0:T(1024)} %param.17) | copy-start | bytes 13828
  411.1 1.3 copy-start.2
  419.7 3.8 copy-start.4
  419.7 3.8 copy-start.11
  428.1 1.8 copy-start.1
  431.0 45.7 %collective-permute-start = (bf16[128,28,128]{0,2,1:T(8,128)(2,1)}, bf16[128,28,128]{0,2,1:T(8,128)(2,1)}, u32[]{:S(2)}, u32[]{:S(2)}) collective-permute-start(bf16[128,28,128]{0,2,1:T(8,128)(2,1)} %fusion.10), channel_id=1, source_target_pairs={{0,1},{1,0},{2,3},{3,2},{4,5},{5,4},{6,7},{7,6},{8,9},{9,8},{10,11... | collective-permute-start | bytes 2752520 | tf_op jit(solution)/shard_map/ppermute | solution.py:164
  476.8 3.4 copy-start
Sparse Core Ops, SparseCore 0:
  21.1 54.4 all-gather.7
  77.4 85.5 all-gather.9
  164.8 37.2 all-gather.11

commit v4 on v3

--- a/solution.py
+++ b/solution.py
@@ -15,6 +15,7 @@
 THETA = 1000000.0
 MASKED = -1e30
 MEMBER = ("y", "zl", "x", "c")
+CHIP_AXES = ("y", "zl", "x")
 
 
 def rope_tables(length, head_size):
@@ -87,16 +88,15 @@
         ],
         axis=0,
     )
-    gathered = lax.all_gather(stacked, "x", axis=0)
-    gathered = lax.all_gather(gathered, "zl", axis=0)
-    gathered = lax.all_gather(gathered, "y", axis=0)
-    gathered = lax.all_gather(gathered, "c", axis=3)
+    chip_gathered = lax.all_gather(stacked, CHIP_AXES, axis=0)
+    picked = jnp.take(embed_table, all_ids.reshape(-1), axis=1)
+    after_pick = picked[0, 0] * jnp.zeros((), picked.dtype)
+    gathered = lax.all_gather(chip_gathered + after_pick, "c", axis=1)
     gathered = gathered.reshape((member_count,) + stacked.shape)
     block_qkv = gathered[:, :feature_rows, :qkv_cols]
     block_out = gathered[:, :feature_rows, qkv_cols:]
     right_cols = gathered[:, feature_rows:, :qkv_cols].reshape(population, qkv_cols)
     left_cols = gathered[:, feature_rows:, qkv_cols:].reshape(population, out_cols)
-    picked = jnp.take(embed_table, all_ids.reshape(-1), axis=1)
     token_block = row_count
     factor_width = 2 * feature_rows * members
     factors = jnp.concatenate(

time: 491 us -> 560 us (1.14)
  starting transfers between devices: 26.9 us -> 70.8 us
  waiting for transfers between devices: 221 us -> 246 us
  blocking collectives: 12.8 us -> 0 us
  other arithmetic: 14.7 us -> 23.2 us
    all_to_all x1, starting transfers between devices: 12.5 us -> 53.2 us  [on_device(): lax.all_to_all(combined, MEMBER, split_axis=1, concat_axis=0, tiled=True)]
    all_gather x3 -> x2, waiting for transfers between devices: 142 us -> 168 us  [the longest x1 168 us: on_device(): chip_gathered = lax.all_gather(stacked, CHIP_AXES, axis=0)]
    all_gather x1 -> x0, blocking collectives: 12.8 us -> none  [on_device(): gathered = lax.all_gather(stacked, 'x', axis=0)]
    add x0 -> x1, other arithmetic: none -> 7.14 us  [on_device(): gathered = lax.all_gather(chip_gathered + after_pick, 'c', axis=1)]
    unnamed x30 -> x26, local copies, waits for them, and re-layouts: 20.8 us -> 20.3 us
  transfers between devices with their start and end apart: 6 -> 5, of which waited for: 4 -> 3; matrix products, arithmetic and copies ran while one was open for 34% -> 30% of each run, Pallas kernels for 0% -> 0%
where the time goes in v4:
time: 560 us; the launch traced here: 558 us
  waiting for transfers between devices  246 us (44%)
  local copies, waits for them, and re-layouts  180 us (32%)
  starting transfers between devices  70.8 us (13%)
  other arithmetic  23.2 us (4%)
  matrix products  20.4 us (4%)
  between operations  18.4 us (3%)
    all_gather x1, waiting for transfers between devices, on_device(): chip_gathered = lax.all_gather(stacked, CHIP_AXES, axis=0)  168 us
    gather x2, local copies, waits for them, and re-layouts, on_device(): picked = jnp.take(embed_table, all_ids.reshape(-1), axis=1)  127 us
    all_to_all x1, starting transfers between devices, on_device(): lax.all_to_all(combined, MEMBER, split_axis=1, concat_axis=0, tiled=True)  53.2 us
    all_to_all x1, waiting for transfers between devices, on_device(): lax.all_to_all(combined, MEMBER, split_axis=1, concat_axis=0, tiled=True)  46.7 us
    ppermute x1, waiting for transfers between devices, on_device(): lax.ppermute(sent_term.astype(jnp.bfloat16), 'mp', perm=[(0, 1), (1, 0)])  30.5 us
    unnamed x26, local copies, waits for them, and re-layouts  20.3 us
    all_to_all x1, starting transfers between devices, on_device(): lax.all_to_all(spread_ids, MEMBER, split_axis=0, concat_axis=0, tiled=True)  13.8 us
  transfers between devices with their start and end apart: 5, of which 3 were waited for; matrix products, arithmetic and copies ran while one was open for 30% of the time, Pallas kernels for 0%

profile of v4, /device:TPU:1, one launch (start us, length us, event | category | flops | bytes accessed | tf_op | source)
XLA Modules:
  0.0 558.5 jit_solution(4233649058326469810)
XLA Ops:
  7.2 1.6 maximum_maximum_fusion
  11.1 13.8 %all-to-all-start = ((s32[128,4,65]{2,1,0:T(4,128)}), s32[128,4,65]{2,1,0:T(4,128)S(1)}, u32[]{:S(2)}, u32[]{:S(2)}) async-start(s32[128,4,65]{2,1,0:T(4,128)} %broadcast_in_dim.27), calls=%async_computation | async-start | bytes 524288 | tf_op jit(solution)/shard_map/all_to_all | solution.py:81
  25.0 15.7 %copy.65 = bf16[28,76032]{0,1:T(8,128)(2,1)} copy(bf16[28,76032]{1,0:T(8,128)(2,1)} %param.14) | data formatting | bytes 8515584 | tf_op args[2]
  41.3 119.1 %gather_fusion = bf16[32768,28]{1,0:T(8,128)(2,1)} fusion(bf16[28,76032]{0,1:T(8,128)(2,1)} %copy.65, s32[32768]{0:T(1024)S(1)} %broadcast_clamp_fusion), kind=kCustom, calls=%fused_computation | custom fusion | bytes 3801088 | tf_op jit(solution)/shard_map/jit(_take)/gather | solution.py:92
  160.4 1.1 slice.78
  163.4 168.5 %all-gather.5.cloned.1.call-done = bf16[2048,2048]{1,0:T(8,128)(2,1)} async-done(((bf16[32,2048]{1,0:T(8,128)(2,1)}), bf16[2048,2048]{1,0:T(8,128)(2,1)}) %all-gather.5.cloned.1.call-update) | async-done | bytes 8388624 | tf_op jit(solution)/shard_map/all_gather | solution.py:91
  331.9 7.1 %broadcast_add_fusion = bf16[2048,2048]{1,0:T(8,128)(2,1)} fusion(bf16[2048,2048]{1,0:T(8,128)(2,1)} %all-gather.5.cloned.1.call-done, bf16[]{:T(256)} %bitcast.10), kind=kLoop, calls=%fused_computation.5 | loop fusion | flops 4194304 | bytes 16777218 | tf_op jit(solution)/shard_map/add | solution.py:94
  341.0 7.6 %copy.66 = bf16[28,128,256]{2,0,1:T(8,128)(2,1)S(1)} copy(bf16[28,128,256]{0,2,1:T(8,128)(2,1)} %bitcast.124) | data formatting | bytes 3670016 | tf_op jit(solution)/shard_map/jit(_take)/gather | solution.py:92
  349.0 1.8 pad_maximum_fusion
  350.8 53.2 %all-to-all-start.1 = ((bf16[29,128,256]{2,0,1:T(8,128)(2,1)}), bf16[29,128,256]{2,0,1:T(8,128)(2,1)}, u32[]{:S(2)}, u32[]{:S(2)}) async-start(bf16[29,128,256]{2,0,1:T(8,128)(2,1)} %pad_maximum_fusion), calls=%async_computation.1 | async-start | bytes 4194304 | tf_op jit(solution)/shard_map/all_to_all | solution.py:112
  408.8 46.7 %all-to-all-done.1 = bf16[29,128,256]{2,0,1:T(8,128)(2,1)} async-done(((bf16[29,128,256]{2,0,1:T(8,128)(2,1)}), bf16[29,128,256]{2,0,1:T(8,128)(2,1)}, u32[]{:S(2)}, u32[]{:S(2)}) %all-to-all-start.1) | async-done | bytes 1900576 | tf_op jit(solution)/shard_map/all_to_all | solution.py:112
  455.6 3.8 copy.70
  460.5 1.2 copy-done.3
  462.3 8.0 %slice.80 = bf16[128,28,1152]{2,1,0:T(8,128)(2,1)} slice(bf16[128,32,2048]{2,1,0:T(8,128)(2,1)} %bitcast.117), slice={[0:128], [0:28], [0:1152]} | slice | bytes 16515072 | tf_op jit(solution)/shard_map/slice | solution.py:96
  470.4 9.6 %fusion = f32[256,1152,1]{1,0,2:T(8,128)S(1)} fusion(bf16[128,28,256]{0,2,1:T(8,128)(2,1)} %copy-done.3, bf16[128,28,1152]{2,1,0:T(8,128)(2,1)} %slice.80), kind=kOutput, calls=%fused_computation.1 | convolution fusion | flops 2113929216 | bytes 11272192 | tf_op jit(solution)/shard_map/abt,abn->tn/dot_general | solution.py:122
  481.6 1.3 reshape.221
  483.8 1.5 fusion.37
  485.4 1.2 fusion.7
  487.0 1.3 dot_general.30
  488.8 3.7 slice.79
  492.8 4.4 multiply_add_fusion
  497.3 1.8 copy-done.1
  499.0 1.1 fusion.10
  500.2 3.7 collective-permute-start
  504.6 2.3 slice_convert_fusion
  506.9 2.3 slice.91
  509.1 2.0 slice.93
  511.9 1.4 convolution_multiply_fusion.2
  513.2 1.5 convolution_multiply_fusion
  514.7 30.5 %collective-permute-done = bf16[128,28,128]{0,2,1:T(8,128)(2,1)} collective-permute-done((bf16[128,28,128]{0,2,1:T(8,128)(2,1)}, bf16[128,28,128]{0,2,1:T(8,128)(2,1)}, u32[]{:S(2)}, u32[]{:S(2)}) %collective-permute-start) | collective-permute-done | bytes 917536 | tf_op jit(solution)/shard_map/ppermute | solution.py:164
  545.2 2.9 multiply_reduce_fusion.2
  548.6 2.3 multiply_reduce_fusion.1
  (86 shorter events, 15.7 us)
Async XLA Ops:
  7.2 324.7 %all-gather.5.cloned.1.call-start = ((), (), s32[]{:S(2)}) async-start(), calls=%async_computation.2 | async-start | bytes 8519680 | tf_op jit(solution)/shard_map/all_gather | solution.py:91
  11.1 29.6 %all-to-all-start = ((s32[128,4,65]{2,1,0:T(4,128)}), s32[128,4,65]{2,1,0:T(4,128)S(1)}, u32[]{:S(2)}, u32[]{:S(2)}) async-start(s32[128,4,65]{2,1,0:T(4,128)} %broadcast_in_dim.27), calls=%async_computation | async-start | bytes 524288 | tf_op jit(solution)/shard_map/all_to_all | solution.py:81
  24.9 437.4 %all-gather.7.cloned.1.call-start = ((), (), s32[]{:S(2)}) async-start(), calls=%async_computation.3 | async-start | bytes 25165824 | tf_op jit(solution)/shard_map/all_gather | solution.py:94
  339.0 0.7 copy-start.7
  339.0 1.2 copy-start.5
  350.8 53.5 %copy-start.6 = (bf16[4,1152]{1,0:T(4,128)(2,1)S(1)}, bf16[4,1152]{1,0:T(4,128)(2,1)}, u32[]{:S(2)}) copy-start(bf16[4,1152]{1,0:T(4,128)(2,1)} %param.21) | copy-start | bytes 27652
  350.8 53.6 %copy-start.8 = (f32[3584]{0:T(1024)S(1)}, f32[3584]{0:T(1024)}, u32[]{:S(2)}) copy-start(f32[3584]{0:T(1024)} %param.15) | copy-start | bytes 43012
  350.8 54.1 %copy-start.9 = (f32[3584]{0:T(1024)S(1)}, f32[3584]{0:T(1024)}, u32[]{:S(2)}) copy-start(f32[3584]{0:T(1024)} %param.19) | copy-start | bytes 43012
  350.8 104.7 %all-to-all-start.1 = ((bf16[29,128,256]{2,0,1:T(8,128)(2,1)}), bf16[29,128,256]{2,0,1:T(8,128)(2,1)}, u32[]{:S(2)}, u32[]{:S(2)}) async-start(bf16[29,128,256]{2,0,1:T(8,128)(2,1)} %pad_maximum_fusion), calls=%async_computation.1 | async-start | bytes 4194304 | tf_op jit(solution)/shard_map/all_to_all | solution.py:112
  460.5 1.2 copy-start.3
  470.4 9.7 %copy-start.10 = (f32[1152]{0:T(1024)S(1)}, f32[1152]{0:T(1024)}, u32[]{:S(2)}) copy-start(f32[1152]{0:T(1024)} %param.17) | copy-start | bytes 13828
  480.2 1.3 copy-start.2
  488.8 3.8 copy-start.4
  488.8 3.8 copy-start.11
  497.3 1.8 copy-start.1
  500.2 45.0 %collective-permute-start = (bf16[128,28,128]{0,2,1:T(8,128)(2,1)}, bf16[128,28,128]{0,2,1:T(8,128)(2,1)}, u32[]{:S(2)}, u32[]{:S(2)}) collective-permute-start(bf16[128,28,128]{0,2,1:T(8,128)(2,1)} %fusion.10), channel_id=1, source_target_pairs={{0,1},{1,0},{2,3},{3,2},{4,5},{5,4},{6,7},{7,6},{8,9},{9,8},{10,11... | collective-permute-start | bytes 2752520 | tf_op jit(solution)/shard_map/ppermute | solution.py:164
  545.2 3.4 copy-start
Sparse Core Ops, SparseCore 0:
  10.3 321.5 all-gather.4
  339.2 76.8 all-gather.6

commit v5 on v2

--- a/solution.py
+++ b/solution.py
@@ -87,8 +87,9 @@
         axis=0,
     )
     gathered = lax.all_gather(stacked, "member", axis=0)
-    block_qkv = gathered[:, :feature_rows, :qkv_cols]
-    block_out = gathered[:, :feature_rows, qkv_cols:]
+    block_rows = gathered.shape[1]
+    block_qkv = gathered[:, :, :qkv_cols]
+    block_out = gathered[:, :, qkv_cols:]
     right_cols = gathered[:, feature_rows:, :qkv_cols].reshape(population, qkv_cols)
     left_cols = gathered[:, feature_rows:, qkv_cols:].reshape(population, out_cols)
     picked = jnp.take(embed_table, all_ids.reshape(-1), axis=1)
@@ -103,20 +104,27 @@
     )
     factors = factors.transpose(1, 0, 2).reshape(member_count, factor_width)
     factors = jnp.pad(factors, ((0, 0), (0, token_block - factor_width))).reshape(1, -1)
-    combined = jnp.concatenate([picked, factors], axis=0)
+    spare = jnp.zeros((block_rows - feature_rows - 1, picked.shape[1]), picked.dtype)
+    combined = jnp.concatenate([picked, factors, spare], axis=0)
     arrived = lax.all_to_all(combined, "member", split_axis=1, concat_axis=0, tiled=True)
-    arrived = arrived.reshape(member_count, feature_rows + 1, token_block)
-    embedded = arrived[:, :feature_rows, :]
+    arrived = arrived.reshape(member_count, block_rows, token_block)
     factor_cols = arrived[:, feature_rows, :factor_width].reshape(population, 2 * feature_rows)
+    real_row = (jnp.arange(block_rows) < feature_rows)[None, :, None]
     left_rows = factor_cols[:, :feature_rows]
     right_rows = factor_cols[:, feature_rows:]
-    features = embedded.astype(jnp.float32)
-    inverse_rms = lax.rsqrt(jnp.mean(features * features, axis=(0, 1), keepdims=True) + EPSILON)
-    gain = norm_gain.reshape(member_count, feature_rows, 1)
+    feature_count = member_count * feature_rows
+    features = jnp.where(real_row, arrived.astype(jnp.float32), 0.0)
+    inverse_rms = lax.rsqrt(
+        jnp.sum(features * features, axis=(0, 1), keepdims=True) / feature_count + EPSILON
+    )
+    row_pad = ((0, 0), (0, block_rows - feature_rows))
+    gain = jnp.pad(norm_gain.reshape(member_count, feature_rows), row_pad)[:, :, None]
     normed = (features * inverse_rms * gain).astype(jnp.bfloat16)
     base_proj = jnp.einsum("abt,abn->tn", normed, block_qkv, preferred_element_type=jnp.float32)
-    normed_members = normed.reshape(member_count, feature_rows, members, length)
-    left_blocks = qkv_left.reshape(members, member_count, feature_rows)
+    normed_members = normed.reshape(member_count, block_rows, members, length)
+    left_blocks = jnp.pad(
+        qkv_left.reshape(members, member_count, feature_rows), ((0, 0),) + row_pad
+    )
     coef_in = jnp.einsum(
         "abms,mab->ms", normed_members, left_blocks, preferred_element_type=jnp.float32
     )
@@ -148,9 +156,9 @@
         "tc,abc->abt", flat_context, block_out, preferred_element_type=jnp.float32
     )
     right_blocks = out_right.reshape(members, member_count, feature_rows).astype(jnp.float32)
-    head_term = partial_out.reshape(member_count, feature_rows, members, length) + SIGMA * (
-        right_blocks.transpose(1, 2, 0)[:, :, :, None] * coef_out[None, None, :, :]
-    )
+    head_term = partial_out[:, :feature_rows].reshape(
+        member_count, feature_rows, members, length
+    ) + SIGMA * (right_blocks.transpose(1, 2, 0)[:, :, :, None] * coef_out[None, None, :, :])
     share = members // mp_size
     head_term = head_term.reshape(member_count, feature_rows, mp_size, share * length)
     mp_index = lax.axis_index("mp")
@@ -158,7 +166,7 @@
     sent_term = lax.dynamic_index_in_dim(head_term, 1 - mp_index, axis=2, keepdims=False)
     got_term = lax.ppermute(sent_term.astype(jnp.bfloat16), "mp", perm=[(0, 1), (1, 0)])
     own_embed = lax.dynamic_index_in_dim(
-        features.reshape(member_count, feature_rows, mp_size, share * length),
+        features[:, :feature_rows].reshape(member_count, feature_rows, mp_size, share * length),
         mp_index,
         axis=2,
         keepdims=False,

time: 344 us -> 357 us (1.038)
  the two profiles are of different devices: /device:TPU:37 before, /device:TPU:26 now
where the time goes in v5:
time: 357 us; the launch traced here: 356 us
  local copies, waits for them, and re-layouts  185 us (52%)
  waiting for transfers between devices  79.5 us (22%)
  starting transfers between devices  29.5 us (8%)
  matrix products  25.4 us (7%)
  other arithmetic  18.8 us (5%)
  between operations  17.1 us (5%)
    gather x2, local copies, waits for them, and re-layouts, on_device(): picked = jnp.take(embed_table, all_ids.reshape(-1), axis=1)  127 us
    all_to_all x1, waiting for transfers between devices, on_device(): lax.all_to_all(combined, 'member', split_axis=1, concat_axis=0, tiled=True)  53.6 us
    ppermute x1, waiting for transfers between devices, on_device(): lax.ppermute(sent_term.astype(jnp.bfloat16), 'mp', perm=[(0, 1), (1, 0)])  25.9 us
    unnamed x31, local copies, waits for them, and re-layouts  20.1 us
    all_to_all x1, starting transfers between devices, on_device(): lax.all_to_all(spread_ids, 'member', split_axis=0, concat_axis=0, tiled=T...  13.1 us
    all_to_all x1, starting transfers between devices, on_device(): lax.all_to_all(combined, 'member', split_axis=1, concat_axis=0, tiled=True)  12.3 us
    dot_general x1, matrix products, on_device(): jnp.einsum('abt,abn->tn', normed, block_qkv, preferred_element_type=jnp.f...  10.8 us
    slice x1, local copies, waits for them, and re-layouts, on_device(): block_qkv = gathered[:, :, :qkv_cols]  8.05 us
  transfers between devices with their start and end apart: 4, of which 2 were waited for; matrix products, arithmetic and copies ran while one was open for 49% of the time, Pallas kernels for 0%

profile of v5, /device:TPU:26, one launch (start us, length us, event | category | flops | bytes accessed | tf_op | source)
XLA Modules:
  0.0 355.7 jit_solution(1046332328116540648)
XLA Ops:
  7.2 1.6 maximum_maximum_fusion.1
  11.1 13.1 %all-to-all-start = ((s32[128,4,65]{2,1,0:T(4,128)}), s32[128,4,65]{2,1,0:T(4,128)S(1)}, u32[]{:S(2)}, u32[]{:S(2)}) async-start(s32[128,4,65]{2,1,0:T(4,128)} %broadcast_in_dim.38), calls=%async_computation | async-start | bytes 524288 | tf_op jit(solution)/shard_map/all_to_all | solution.py:79
  24.2 15.8 %copy.68 = bf16[28,76032]{0,1:T(8,128)(2,1)} copy(bf16[28,76032]{1,0:T(8,128)(2,1)} %param.14) | data formatting | bytes 8515584 | tf_op args[2]
  41.7 119.3 %gather_fusion = bf16[32768,28]{1,0:T(8,128)(2,1)} fusion(bf16[28,76032]{0,1:T(8,128)(2,1)} %copy.68, s32[32768]{0:T(1024)S(1)} %broadcast_clamp_fusion), kind=kCustom, calls=%fused_computation | custom fusion | bytes 3801088 | tf_op jit(solution)/shard_map/jit(_take)/gather | solution.py:95
  161.1 7.6 %copy.69 = bf16[28,128,256]{2,0,1:T(8,128)(2,1)S(1)} copy(bf16[28,128,256]{0,2,1:T(8,128)(2,1)} %bitcast.105) | data formatting | bytes 3670016 | tf_op jit(solution)/shard_map/jit(_take)/gather | solution.py:95
  169.1 2.4 maximum_maximum_fusion
  171.5 12.3 %all-to-all-start.1 = ((bf16[32,128,256]{2,0,1:T(8,128)(2,1)}), bf16[32,128,256]{2,0,1:T(8,128)(2,1)}, u32[]{:S(2)}, u32[]{:S(2)}) async-start(bf16[32,128,256]{2,0,1:T(8,128)(2,1)} %maximum_maximum_fusion), calls=%async_computation.1 | async-start | bytes 4194304 | tf_op jit(solution)/shard_map/all_to_all | solution.py:109
  185.8 53.6 %all-to-all-done.1 = bf16[32,128,256]{2,0,1:T(8,128)(2,1)} async-done(((bf16[32,128,256]{2,0,1:T(8,128)(2,1)}), bf16[32,128,256]{2,0,1:T(8,128)(2,1)}, u32[]{:S(2)}, u32[]{:S(2)}) %all-to-all-start.1) | async-done | bytes 2097184 | tf_op jit(solution)/shard_map/all_to_all | solution.py:109
  239.4 3.4 copy.73
  242.9 2.8 convert_select_fusion
  246.7 1.3 copy-done.3
  248.6 8.0 %slice.78 = bf16[128,32,1152]{2,1,0:T(8,128)(2,1)} slice(bf16[128,32,2048]{2,1,0:T(8,128)(2,1)} %bitcast.97), slice={[0:128], [0:32], [0:1152]} | slice | bytes 18874368 | tf_op jit(solution)/shard_map/slice | solution.py:91
  256.7 10.8 %fusion = f32[256,1152,1]{1,0,2:T(8,128)S(1)} fusion(bf16[128,32,256]{0,2,1:T(8,128)(2,1)} %copy-done.3, bf16[128,32,1152]{2,1,0:T(8,128)(2,1)} %slice.78), kind=kOutput, calls=%fused_computation.1 | convolution fusion | flops 2415919104 | bytes 12713984 | tf_op jit(solution)/shard_map/abt,abn->tn/dot_general | solution.py:123
  267.7 1.1 slice.83
  269.1 6.6 %slice.77 = bf16[128,32,896]{2,1,0:T(8,128)(2,1)} slice(bf16[128,32,2048]{2,1,0:T(8,128)(2,1)} %bitcast.98), slice={[0:128], [0:32], [1152:2048]} | slice | bytes 14680064 | tf_op jit(solution)/shard_map/slice | solution.py:92
  275.7 1.3 reshape.227
  278.2 1.5 fusion.38
  279.9 1.2 fusion.8
  282.0 1.3 reshape.230
  283.3 1.3 fusion.35
  284.7 7.2 %fusion.2 = f32[128,28,256]{0,2,1:T(8,128)S(1)} fusion(bf16[256,896,1]{1,0,2:T(8,128)(2,1)S(1)} %reshape.248, bf16[128,32,896]{2,1,0:T(8,128)(2,1)} %slice.77), kind=kOutput, calls=%fused_computation.3 | convolution fusion | flops 1644167168 | bytes 11468800 | tf_op jit(solution)/shard_map/reshape | solution.py:159
  292.1 1.2 fusion.5
  293.3 1.8 copy-done
  296.2 4.2 %collective-permute-start = (bf16[128,28,128]{0,2,1:T(8,128)(2,1)}, bf16[128,28,128]{0,2,1:T(8,128)(2,1)}, u32[]{:S(2)}, u32[]{:S(2)}) collective-permute-start(bf16[128,28,128]{0,2,1:T(8,128)(2,1)} %fusion.11), channel_id=1, source_target_pairs={{0,1},{1,0},{2,3},{3,2},{4,5},{5,4},{6,7},{7,6},{8,9},{9,8},{10,11... | collective-permute-start | bytes 2752520 | tf_op jit(solution)/shard_map/ppermute | solution.py:167
  304.4 4.2 %slice.76 = f32[128,28,256]{0,2,1:T(8,128)} slice(f32[128,32,256]{0,2,1:T(8,128)} %get-tuple-element.5), slice={[0:128], [0:28], [0:256]} | slice | bytes 7340032 | tf_op jit(solution)/shard_map/slice | solution.py:169
  308.9 2.3 slice.89
  311.2 2.0 slice.91
  313.7 1.4 convolution_multiply_fusion.2
  315.1 1.5 convolution_multiply_fusion
  316.6 25.9 %collective-permute-done = bf16[128,28,128]{0,2,1:T(8,128)(2,1)} collective-permute-done((bf16[128,28,128]{0,2,1:T(8,128)(2,1)}, bf16[128,28,128]{0,2,1:T(8,128)(2,1)}, u32[]{:S(2)}, u32[]{:S(2)}) %collective-permute-start) | collective-permute-done | bytes 917536 | tf_op jit(solution)/shard_map/ppermute | solution.py:167
  342.5 2.9 multiply_reduce_fusion.2
  345.9 2.3 multiply_reduce_fusion.1
  (89 shorter events, 15.3 us)
Async XLA Ops:
  7.2 241.5 %all-gather.3.cloned.1.call-start = ((), (), s32[]{:S(2)}) async-start(), calls=%async_computation.2 | async-start | bytes 16908288 | tf_op jit(solution)/shard_map/all_gather | solution.py:89
  11.1 30.1 %all-to-all-start = ((s32[128,4,65]{2,1,0:T(4,128)}), s32[128,4,65]{2,1,0:T(4,128)S(1)}, u32[]{:S(2)}, u32[]{:S(2)}) async-start(s32[128,4,65]{2,1,0:T(4,128)} %broadcast_in_dim.38), calls=%async_computation | async-start | bytes 524288 | tf_op jit(solution)/shard_map/all_to_all | solution.py:79
  24.2 15.8 %copy-start.8 = (bf16[4,3584]{1,0:T(4,128)(2,1)S(1)}, bf16[4,3584]{1,0:T(4,128)(2,1)}, u32[]{:S(2)}) copy-start(bf16[4,3584]{1,0:T(4,128)(2,1)} %param.20) | copy-start | bytes 86020
  24.2 16.3 %copy-start.9 = (bf16[4,3584]{1,0:T(4,128)(2,1)S(1)}, bf16[4,3584]{1,0:T(4,128)(2,1)}, u32[]{:S(2)}) copy-start(bf16[4,3584]{1,0:T(4,128)(2,1)} %param.23) | copy-start | bytes 86020
  171.5 12.3 %copy-start.7 = (bf16[4,1152]{1,0:T(4,128)(2,1)S(1)}, bf16[4,1152]{1,0:T(4,128)(2,1)}, u32[]{:S(2)}) copy-start(bf16[4,1152]{1,0:T(4,128)(2,1)} %param.21) | copy-start | bytes 27652
  171.5 12.3 %copy-start.10 = (f32[3584]{0:T(1024)S(1)}, f32[3584]{0:T(1024)}, u32[]{:S(2)}) copy-start(f32[3584]{0:T(1024)} %param.15) | copy-start | bytes 43012
  171.5 67.9 %all-to-all-start.1 = ((bf16[32,128,256]{2,0,1:T(8,128)(2,1)}), bf16[32,128,256]{2,0,1:T(8,128)(2,1)}, u32[]{:S(2)}, u32[]{:S(2)}) async-start(bf16[32,128,256]{2,0,1:T(8,128)(2,1)} %maximum_maximum_fusion), calls=%async_computation.1 | async-start | bytes 4194304 | tf_op jit(solution)/shard_map/all_to_all | solution.py:109
  246.7 1.3 copy-start.3
  256.7 10.8 %copy-start.12 = (f32[1152]{0:T(1024)S(1)}, f32[1152]{0:T(1024)}, u32[]{:S(2)}) copy-start(f32[1152]{0:T(1024)} %param.17) | copy-start | bytes 13828
  267.7 1.4 copy-start.2
  277.0 0.8 copy-start.4
  277.1 0.8 copy-start.5
  281.1 2.2 copy-start.13
  284.6 7.2 %copy-start.6 = (f32[128,28,4]{0,2,1:T(4,128)S(1)}, f32[128,28,4]{0,2,1:T(4,128)}, u32[]{:S(2)}) copy-start(f32[128,28,4]{0,2,1:T(4,128)} %copy.80) | copy-start | bytes 172036
  292.1 8.2 %copy-start.11 = (f32[3584]{0:T(1024)S(1)}, f32[3584]{0:T(1024)}, u32[]{:S(2)}) copy-start(f32[3584]{0:T(1024)} %param.19) | copy-start | bytes 43012
  293.3 1.8 copy-start
  296.2 46.3 %collective-permute-start = (bf16[128,28,128]{0,2,1:T(8,128)(2,1)}, bf16[128,28,128]{0,2,1:T(8,128)(2,1)}, u32[]{:S(2)}, u32[]{:S(2)}) collective-permute-start(bf16[128,28,128]{0,2,1:T(8,128)(2,1)} %fusion.11), channel_id=1, source_target_pairs={{0,1},{1,0},{2,3},{3,2},{4,5},{5,4},{6,7},{7,6},{8,9},{9,8},{10,11... | collective-permute-start | bytes 2752520 | tf_op jit(solution)/shard_map/ppermute | solution.py:167
  342.5 3.4 copy-start.1
Sparse Core Ops, SparseCore 0:
  10.4 228.7 all-gather.2

commit v6 on v2

--- a/solution.py
+++ b/solution.py
@@ -1,6 +1,7 @@
 import math
 
 import jax
+import numpy as np
 import jax.numpy as jnp
 from jax import lax
 from jax.sharding import PartitionSpec as P
@@ -18,11 +19,14 @@
 
 def rope_tables(length, head_size):
     halfway = head_size // 2
-    inverse = THETA ** (-(jnp.arange(halfway, dtype=jnp.float32) * 2.0 / head_size))
-    places = jnp.arange(length, dtype=jnp.float32)
-    angles = places[:, None] * inverse[None, :]
-    angles = jnp.concatenate([angles, angles], axis=1)
-    return (jnp.cos(angles), jnp.sin(angles))
+    steps = np.arange(halfway, dtype=np.float32) * np.float32(2.0) / np.float32(head_size)
+    inverse = np.power(np.float32(THETA), -steps).astype(np.float32)
+    places = np.arange(length, dtype=np.float32)
+    angles = (places[:, None] * inverse[None, :]).astype(np.float32)
+    angles = np.concatenate([angles, angles], axis=1).astype(np.float64)
+    cosine = np.cos(angles).astype(np.float32)
+    sine_table = np.sin(angles).astype(np.float32)
+    return (jnp.asarray(cosine), jnp.asarray(sine_table))
 
 
 def rotate(states, cosine, sine_table):
@@ -91,7 +95,7 @@
     block_out = gathered[:, :feature_rows, qkv_cols:]
     right_cols = gathered[:, feature_rows:, :qkv_cols].reshape(population, qkv_cols)
     left_cols = gathered[:, feature_rows:, qkv_cols:].reshape(population, out_cols)
-    picked = jnp.take(embed_table, all_ids.reshape(-1), axis=1)
+    picked = embed_table.at[:, all_ids.reshape(-1)].get(mode="promise_in_bounds")
     token_block = row_count
     factor_width = 2 * feature_rows * members
     factors = jnp.concatenate(

time: 344 us -> 345 us (level)
  the two profiles are of different devices: /device:TPU:37 before, /device:TPU:1 now
where the time goes in v6:
time: 345 us; the launch traced here: 341 us
  local copies, waits for them, and re-layouts  178 us (52%)
  waiting for transfers between devices  81.5 us (24%)
  starting transfers between devices  28.6 us (8%)
  matrix products  20.4 us (6%)
  between operations  17.1 us (5%)
  other arithmetic  15.5 us (4%)
    gather x1, local copies, waits for them, and re-layouts, on_device(): embed_table.at[:, all_ids.reshape(-1)].get(mode='promise_in_bounds')  119 us
    all_to_all x1, waiting for transfers between devices, on_device(): lax.all_to_all(combined, 'member', split_axis=1, concat_axis=0, tiled=True)  47 us
    ppermute x1, waiting for transfers between devices, on_device(): lax.ppermute(sent_term.astype(jnp.bfloat16), 'mp', perm=[(0, 1), (1, 0)])  28.5 us
    unnamed x29, local copies, waits for them, and re-layouts  19.7 us
    all_to_all x1, starting transfers between devices, on_device(): lax.all_to_all(spread_ids, 'member', split_axis=0, concat_axis=0, tiled=T...  13.8 us
    all_to_all x1, starting transfers between devices, on_device(): lax.all_to_all(combined, 'member', split_axis=1, concat_axis=0, tiled=True)  12.4 us
    dot_general x1, matrix products, on_device(): jnp.einsum('abt,abn->tn', normed, block_qkv, preferred_element_type=jnp.f...  9.64 us
    slice x1, local copies, waits for them, and re-layouts, on_device(): block_qkv = gathered[:, :feature_rows, :qkv_cols]  8.03 us
  transfers between devices with their start and end apart: 4, of which 3 were waited for; matrix products, arithmetic and copies ran while one was open for 49% of the time, Pallas kernels for 0%

profile of v6, /device:TPU:1, one launch (start us, length us, event | category | flops | bytes accessed | tf_op | source)
XLA Modules:
  0.0 340.7 jit_solution(393849501792371151)
XLA Ops:
  7.2 1.6 maximum_maximum_fusion
  11.1 13.8 %all-to-all-start = ((s32[128,4,65]{2,1,0:T(4,128)}), s32[128,4,65]{2,1,0:T(4,128)S(1)}, u32[]{:S(2)}, u32[]{:S(2)}) async-start(s32[128,4,65]{2,1,0:T(4,128)} %broadcast_in_dim.11), calls=%async_computation | async-start | bytes 524288 | tf_op jit(solution)/shard_map/all_to_all | solution.py:83
  25.0 15.7 %copy.62 = bf16[28,76032]{0,1:T(8,128)(2,1)} copy(bf16[28,76032]{1,0:T(8,128)(2,1)} %param.16) | data formatting | bytes 8515584 | tf_op args[2]
  42.2 119.3 %gather_fusion = bf16[32768,28]{1,0:T(8,128)(2,1)} fusion(bf16[28,76032]{0,1:T(8,128)(2,1)} %copy.62, s32[32768]{0:T(1024)S(1)} %broadcast_clamp_fusion), kind=kCustom, calls=%fused_computation | custom fusion | bytes 3801088 | tf_op jit(solution)/shard_map/gather | solution.py:98
  161.5 7.6 %copy.65 = bf16[28,128,256]{2,0,1:T(8,128)(2,1)S(1)} copy(bf16[28,128,256]{0,2,1:T(8,128)(2,1)} %bitcast.114) | data formatting | bytes 3670016 | tf_op jit(solution)/shard_map/concatenate | solution.py:110
  169.0 1.8 pad_maximum_fusion
  170.9 12.4 %all-to-all-start.1 = ((bf16[29,128,256]{2,0,1:T(8,128)(2,1)}), bf16[29,128,256]{2,0,1:T(8,128)(2,1)}, u32[]{:S(2)}, u32[]{:S(2)}) async-start(bf16[29,128,256]{2,0,1:T(8,128)(2,1)} %pad_maximum_fusion), calls=%async_computation.1 | async-start | bytes 4194304 | tf_op jit(solution)/shard_map/all_to_all | solution.py:111
  184.3 0.8 fusion.18
  187.8 47.0 %all-to-all-done.1 = bf16[29,128,256]{2,0,1:T(8,128)(2,1)} async-done(((bf16[29,128,256]{2,0,1:T(8,128)(2,1)}), bf16[29,128,256]{2,0,1:T(8,128)(2,1)}, u32[]{:S(2)}, u32[]{:S(2)}) %all-to-all-start.1) | async-done | bytes 1900576 | tf_op jit(solution)/shard_map/all_to_all | solution.py:111
  234.8 3.8 %copy.67 = bf16[29,128,256]{1,2,0:T(8,128)(2,1)S(1)} copy(bf16[29,128,256]{2,0,1:T(8,128)(2,1)} %all-to-all-done.1) | data formatting | bytes 3801088 | tf_op jit(solution)/shard_map/all_to_all | solution.py:111
  239.7 1.2 copy-done.3
  241.5 6.0 %all-gather.3.cloned.1.call-done = bf16[4096,2048]{1,0:T(8,128)(2,1)} async-done(((bf16[32,2048]{1,0:T(8,128)(2,1)}), bf16[4096,2048]{1,0:T(8,128)(2,1)}) %all-gather.3.cloned.1.call-update) | async-done | bytes 16777232 | tf_op jit(solution)/shard_map/all_gather | solution.py:93
  247.5 8.0 %slice.74 = bf16[128,28,1152]{2,1,0:T(8,128)(2,1)} slice(bf16[128,32,2048]{2,1,0:T(8,128)(2,1)} %bitcast.108), slice={[0:128], [0:28], [0:1152]} | slice | bytes 16515072 | tf_op jit(solution)/shard_map/slice | solution.py:94
  255.5 9.6 %fusion = f32[256,1152,1]{1,0,2:T(8,128)S(1)} fusion(bf16[128,28,256]{0,2,1:T(8,128)(2,1)} %copy-done.3, bf16[128,28,1152]{2,1,0:T(8,128)(2,1)} %slice.74), kind=kOutput, calls=%fused_computation.1 | convolution fusion | flops 2113929216 | bytes 11272192 | tf_op jit(solution)/shard_map/abt,abn->tn/dot_general | solution.py:121
  265.4 1.1 slice.79
  266.7 1.3 reshape.181
  269.2 1.5 fusion.35
  270.9 1.2 fusion.7
  272.5 1.3 dot_general.30
  274.3 3.7 %slice.73 = bf16[128,28,896]{2,1,0:T(8,128)(2,1)S(1)} slice(bf16[128,32,2048]{2,1,0:T(8,128)(2,1)} %bitcast.109), slice={[0:128], [0:28], [1152:2048]} | slice | bytes 12845056 | tf_op jit(solution)/shard_map/slice | solution.py:95
  278.3 4.4 %multiply_add_fusion = f32[128,28,4,64]{0,3,2,1:T(8,128)S(1)} fusion(bf16[4,64,896,1]{2,1,0,3:T(8,128)(2,1)S(1)} %reshape.202, bf16[128,28,896]{2,1,0:T(8,128)(2,1)S(1)} %slice.73, f32[4,64]{1,0:T(4,128)S(1)} %bitcast.126, f32[128,28,4]{0,2,1:T(4,128)S(1)} %copy.75), kind=kOutput, calls=%fused_computation.5 | convolution fusion | flops 1646919680 | bytes 10609664 | tf_op jit(solution)/shard_map/tc,abc->abt/dot_general | solution.py:151
  282.8 1.8 copy-done.1
  284.5 1.1 fusion.10
  285.7 2.4 collective-permute-start
  288.8 2.3 slice_convert_fusion
  291.1 2.3 slice.85
  293.4 2.0 slice.87
  296.1 1.4 convolution_multiply_fusion.2
  297.5 1.5 convolution_multiply_fusion
  298.9 28.5 %collective-permute-done = bf16[128,28,128]{0,2,1:T(8,128)(2,1)} collective-permute-done((bf16[128,28,128]{0,2,1:T(8,128)(2,1)}, bf16[128,28,128]{0,2,1:T(8,128)(2,1)}, u32[]{:S(2)}, u32[]{:S(2)}) %collective-permute-start) | collective-permute-done | bytes 917536 | tf_op jit(solution)/shard_map/ppermute | solution.py:163
  327.4 2.9 multiply_reduce_fusion.2
  330.9 2.3 multiply_reduce_fusion.1
  (75 shorter events, 11.9 us)
Async XLA Ops:
  7.2 240.3 %all-gather.3.cloned.1.call-start = ((), (), s32[]{:S(2)}) async-start(), calls=%async_computation.2 | async-start | bytes 16908288 | tf_op jit(solution)/shard_map/all_gather | solution.py:93
  11.1 30.7 %all-to-all-start = ((s32[128,4,65]{2,1,0:T(4,128)}), s32[128,4,65]{2,1,0:T(4,128)S(1)}, u32[]{:S(2)}, u32[]{:S(2)}) async-start(s32[128,4,65]{2,1,0:T(4,128)} %broadcast_in_dim.11), calls=%async_computation | async-start | bytes 524288 | tf_op jit(solution)/shard_map/all_to_all | solution.py:83
  24.9 15.7 %copy-start.9 = (bf16[4,3584]{1,0:T(4,128)(2,1)S(1)}, bf16[4,3584]{1,0:T(4,128)(2,1)}, u32[]{:S(2)}) copy-start(bf16[4,3584]{1,0:T(4,128)(2,1)} %param.25) | copy-start | bytes 86020
  24.9 16.2 %copy-start.7 = (bf16[4,3584]{1,0:T(4,128)(2,1)S(1)}, bf16[4,3584]{1,0:T(4,128)(2,1)}, u32[]{:S(2)}) copy-start(bf16[4,3584]{1,0:T(4,128)(2,1)} %param.22) | copy-start | bytes 86020
  170.9 12.7 %copy-start.8 = (bf16[4,1152]{1,0:T(4,128)(2,1)S(1)}, bf16[4,1152]{1,0:T(4,128)(2,1)}, u32[]{:S(2)}) copy-start(bf16[4,1152]{1,0:T(4,128)(2,1)} %param.23) | copy-start | bytes 27652
  170.9 12.7 %copy-start.10 = (f32[3584]{0:T(1024)S(1)}, f32[3584]{0:T(1024)}, u32[]{:S(2)}) copy-start(f32[3584]{0:T(1024)} %param.17) | copy-start | bytes 43012
  170.9 13.2 %copy-start.11 = (f32[3584]{0:T(1024)S(1)}, f32[3584]{0:T(1024)}, u32[]{:S(2)}) copy-start(f32[3584]{0:T(1024)} %param.21) | copy-start | bytes 43012
  170.9 63.9 %all-to-all-start.1 = ((bf16[29,128,256]{2,0,1:T(8,128)(2,1)}), bf16[29,128,256]{2,0,1:T(8,128)(2,1)}, u32[]{:S(2)}, u32[]{:S(2)}) async-start(bf16[29,128,256]{2,0,1:T(8,128)(2,1)} %pad_maximum_fusion), calls=%async_computation.1 | async-start | bytes 4194304 | tf_op jit(solution)/shard_map/all_to_all | solution.py:111
  239.7 1.2 copy-start.3
  255.5 9.7 %copy-start.12 = (f32[1152]{0:T(1024)S(1)}, f32[1152]{0:T(1024)}, u32[]{:S(2)}) copy-start(f32[1152]{0:T(1024)} %param.19) | copy-start | bytes 13828
  265.4 1.3 copy-start.2
  268.1 0.8 copy-start.5
  268.1 0.8 copy-start.6
  274.3 3.8 %copy-start.4 = (bf16[4,64,896]{2,1,0:T(8,128)(2,1)S(1)}, bf16[4,64,896]{2,1,0:T(8,128)(2,1)}, u32[]{:S(2)}) copy-start(bf16[4,64,896]{2,1,0:T(8,128)(2,1)} %dot_general.30) | copy-start | bytes 1376260
  274.3 3.8 %copy-start.13 = (bf16[4,896]{1,0:T(4,128)(2,1)S(1)}, bf16[4,896]{1,0:T(4,128)(2,1)}, u32[]{:S(2)}) copy-start(bf16[4,896]{1,0:T(4,128)(2,1)} %param.24) | copy-start | bytes 21508
  282.7 1.8 copy-start.1
  285.7 41.8 %collective-permute-start = (bf16[128,28,128]{0,2,1:T(8,128)(2,1)}, bf16[128,28,128]{0,2,1:T(8,128)(2,1)}, u32[]{:S(2)}, u32[]{:S(2)}) collective-permute-start(bf16[128,28,128]{0,2,1:T(8,128)(2,1)} %fusion.10), channel_id=1, source_target_pairs={{0,1},{1,0},{2,3},{3,2},{4,5},{5,4},{6,7},{7,6},{8,9},{9,8},{10,11... | collective-permute-start | bytes 2752520 | tf_op jit(solution)/shard_map/ppermute | solution.py:163
  327.4 3.4 %copy-start = (f32[128,28,256]{0,2,1:T(8,128)S(1)}, f32[128,28,256]{0,2,1:T(8,128)}, u32[]{:S(2)}) copy-start(f32[128,28,256]{0,2,1:T(8,128)} %slice_convert_fusion) | copy-start | bytes 11010052
Sparse Core Ops, SparseCore 0:
  10.4 237.0 all-gather.2

commit v7 on v4

--- a/solution.py
+++ b/solution.py
@@ -1,6 +1,7 @@
 import math
 
 import jax
+import numpy as np
 import jax.numpy as jnp
 from jax import lax
 from jax.sharding import PartitionSpec as P
@@ -15,16 +16,19 @@
 THETA = 1000000.0
 MASKED = -1e30
 MEMBER = ("y", "zl", "x", "c")
-CHIP_AXES = ("y", "zl", "x")
+BLOCK_AXES = ("zl", "x", "c")
 
 
 def rope_tables(length, head_size):
     halfway = head_size // 2
-    inverse = THETA ** (-(jnp.arange(halfway, dtype=jnp.float32) * 2.0 / head_size))
-    places = jnp.arange(length, dtype=jnp.float32)
-    angles = places[:, None] * inverse[None, :]
-    angles = jnp.concatenate([angles, angles], axis=1)
-    return (jnp.cos(angles), jnp.sin(angles))
+    steps = np.arange(halfway, dtype=np.float32) * np.float32(2.0) / np.float32(head_size)
+    inverse = np.power(np.float32(THETA), -steps).astype(np.float32)
+    places = np.arange(length, dtype=np.float32)
+    angles = (places[:, None] * inverse[None, :]).astype(np.float32)
+    angles = np.concatenate([angles, angles], axis=1).astype(np.float64)
+    cosine = np.cos(angles).astype(np.float32)
+    sine_table = np.sin(angles).astype(np.float32)
+    return (jnp.asarray(cosine), jnp.asarray(sine_table))
 
 
 def rotate(states, cosine, sine_table):
@@ -88,17 +92,24 @@
         ],
         axis=0,
     )
-    chip_gathered = lax.all_gather(stacked, CHIP_AXES, axis=0)
-    picked = jnp.take(embed_table, all_ids.reshape(-1), axis=1)
-    after_pick = picked[0, 0] * jnp.zeros((), picked.dtype)
-    gathered = lax.all_gather(chip_gathered + after_pick, "c", axis=1)
+    y_count = lax.axis_size("y")
+    spread_rows = jnp.broadcast_to(stacked[None], (y_count,) + stacked.shape)
+    gathered = lax.all_to_all(spread_rows, "y", split_axis=0, concat_axis=0, tiled=True)
+    gathered = lax.all_gather(gathered, BLOCK_AXES, axis=1)
     gathered = gathered.reshape((member_count,) + stacked.shape)
     block_qkv = gathered[:, :feature_rows, :qkv_cols]
     block_out = gathered[:, :feature_rows, qkv_cols:]
     right_cols = gathered[:, feature_rows:, :qkv_cols].reshape(population, qkv_cols)
     left_cols = gathered[:, feature_rows:, qkv_cols:].reshape(population, out_cols)
-    token_block = row_count
+    mp_index = lax.axis_index("mp")
+    share = members // mp_size
+    half_ids = lax.dynamic_slice_in_dim(
+        all_ids.reshape(member_count, members, length), mp_index * share, share, 1
+    )
+    picked = embed_table.at[:, half_ids.reshape(-1)].get(mode="promise_in_bounds")
+    token_block = share * length
     factor_width = 2 * feature_rows * members
+    factor_rows = -(-factor_width // token_block)
     factors = jnp.concatenate(
         [
             qkv_left.reshape(members, member_count, feature_rows),
@@ -107,12 +118,20 @@
         axis=2,
     )
     factors = factors.transpose(1, 0, 2).reshape(member_count, factor_width)
-    factors = jnp.pad(factors, ((0, 0), (0, token_block - factor_width))).reshape(1, -1)
-    combined = jnp.concatenate([picked, factors], axis=0)
+    factors = jnp.pad(factors, ((0, 0), (0, factor_rows * token_block - factor_width)))
+    factors = factors.reshape(member_count, factor_rows, token_block).transpose(1, 0, 2)
+    combined = jnp.concatenate([picked, factors.reshape(factor_rows, -1)], axis=0)
     arrived = lax.all_to_all(combined, MEMBER, split_axis=1, concat_axis=0, tiled=True)
-    arrived = arrived.reshape(member_count, feature_rows + 1, token_block)
-    embedded = arrived[:, :feature_rows, :]
-    factor_cols = arrived[:, feature_rows, :factor_width].reshape(population, 2 * feature_rows)
+    arrived = arrived.reshape(member_count, feature_rows + factor_rows, token_block)
+    own_half = arrived[:, :feature_rows, :]
+    factor_cols = arrived[:, feature_rows:, :].reshape(member_count, factor_rows * token_block)
+    factor_cols = factor_cols[:, :factor_width].reshape(population, 2 * feature_rows)
+    other_half = lax.ppermute(own_half, "mp", perm=[(0, 1), (1, 0)])
+    embedded = jnp.where(
+        mp_index == 0,
+        jnp.concatenate([own_half, other_half], axis=2),
+        jnp.concatenate([other_half, own_half], axis=2),
+    )
     left_rows = factor_cols[:, :feature_rows]
     right_rows = factor_cols[:, feature_rows:]
     features = embedded.astype(jnp.float32)
@@ -156,18 +175,11 @@
     head_term = partial_out.reshape(member_count, feature_rows, members, length) + SIGMA * (
         right_blocks.transpose(1, 2, 0)[:, :, :, None] * coef_out[None, None, :, :]
     )
-    share = members // mp_size
     head_term = head_term.reshape(member_count, feature_rows, mp_size, share * length)
-    mp_index = lax.axis_index("mp")
     own_term = lax.dynamic_index_in_dim(head_term, mp_index, axis=2, keepdims=False)
     sent_term = lax.dynamic_index_in_dim(head_term, 1 - mp_index, axis=2, keepdims=False)
     got_term = lax.ppermute(sent_term.astype(jnp.bfloat16), "mp", perm=[(0, 1), (1, 0)])
-    own_embed = lax.dynamic_index_in_dim(
-        features.reshape(member_count, feature_rows, mp_size, share * length),
-        mp_index,
-        axis=2,
-        keepdims=False,
-    )
+    own_embed = own_half.astype(jnp.float32)
     residual = own_embed + own_term + got_term.astype(jnp.float32)
     inverse_out = lax.rsqrt(jnp.mean(residual * residual, axis=(0, 1), keepdims=True) + EPSILON)
     value_gain = value_weight.reshape(member_count, feature_rows, 1)

time: 560 us -> 307 us (0.55)
  waiting for transfers between devices: 246 us -> 64.4 us
  local copies, waits for them, and re-layouts: 180 us -> 117 us
  blocking collectives: 0 us -> 53.8 us
  starting transfers between devices: 70.8 us -> 22.3 us
  other arithmetic: 23.2 us -> 10.6 us
    all_gather x2 -> x1, waiting for transfers between devices: 168 us -> 0.01 us  [on_device(): gathered = lax.all_gather(gathered, BLOCK_AXES, axis=1)]
    gather x2 -> x1, local copies, waits for them, and re-layouts: 127 us -> 64.8 us  [on_device(): embed_table.at[:, half_ids.reshape(-1)].get(mode='promise_in_bounds')]
    all_to_all x0 -> x2, blocking collectives: none -> 53.8 us  [the longest x1 41 us: on_device(): lax.all_to_all(combined, MEMBER, split_axis=1, concat_axis=0, tiled=True)]
    all_to_all x1 -> x0, starting transfers between devices: 53.2 us -> none  [on_device(): lax.all_to_all(combined, MEMBER, split_axis=1, concat_axis=0, tiled=True)]
    all_to_all x1 -> x0, waiting for transfers between devices: 46.7 us -> none  [on_device(): lax.all_to_all(combined, MEMBER, split_axis=1, concat_axis=0, tiled=True)]
    ppermute x0 -> x1, waiting for transfers between devices: none -> 38.7 us  [on_device(): other_half = lax.ppermute(own_half, 'mp', perm=[(0, 1), (1, 0)])]
    add x1 -> x0, other arithmetic: 7.14 us -> none  [on_device(): gathered = lax.all_gather(chip_gathered + after_pick, 'c', axis=1)]
    unnamed x26 -> x32, local copies, waits for them, and re-layouts: 20.3 us -> 18.4 us
  transfers between devices with their start and end apart: 5 -> 4, of which waited for: 3 -> 2; matrix products, arithmetic and copies ran while one was open for 30% -> 35% of each run, Pallas kernels for 0% -> 0%
where the time goes in v7:
time: 307 us; the launch traced here: 305 us
  local copies, waits for them, and re-layouts  117 us (38%)
  waiting for transfers between devices  64.4 us (21%)
  blocking collectives  53.8 us (18%)
  starting transfers between devices  22.3 us (7%)
  matrix products  20.2 us (7%)
  between operations  17.2 us (6%)
  other arithmetic  10.6 us (3%)
    gather x1, local copies, waits for them, and re-layouts, on_device(): embed_table.at[:, half_ids.reshape(-1)].get(mode='promise_in_bounds')  64.8 us
    all_to_all x1, blocking collectives, on_device(): lax.all_to_all(combined, MEMBER, split_axis=1, concat_axis=0, tiled=True)  41 us
    ppermute x1, waiting for transfers between devices, on_device(): other_half = lax.ppermute(own_half, 'mp', perm=[(0, 1), (1, 0)])  38.7 us
    ppermute x1, waiting for transfers between devices, on_device(): lax.ppermute(sent_term.astype(jnp.bfloat16), 'mp', perm=[(0, 1), (1, 0)])  25.6 us
    unnamed x32, local copies, waits for them, and re-layouts  18.4 us
    all_to_all x1, starting transfers between devices, on_device(): lax.all_to_all(spread_ids, MEMBER, split_axis=0, concat_axis=0, tiled=True)  12.8 us
    all_to_all x1, blocking collectives, on_device(): lax.all_to_all(spread_rows, 'y', split_axis=0, concat_axis=0, tiled=True)  12.8 us
    dot_general x1, matrix products, on_device(): jnp.einsum('abt,abn->tn', normed, block_qkv, preferred_element_type=jnp.f...  9.56 us
  transfers between devices with their start and end apart: 4, of which 2 were waited for; matrix products, arithmetic and copies ran while one was open for 35% of the time, Pallas kernels for 0%

profile of v7, /device:TPU:1, one launch (start us, length us, event | category | flops | bytes accessed | tf_op | source)
XLA Modules:
  0.0 305.3 jit_solution(9294373821871471503)
XLA Ops:
  7.2 1.0 maximum_maximum_fusion
  8.3 12.8 %all_to_all.23 = bf16[4,32,2048]{2,1,0:T(8,128)(2,1)} all-to-all(bf16[4,32,2048]{2,1,0:T(8,128)(2,1)S(1)} %broadcast_in_dim.14), channel_id=1, replica_groups=mesh['y'=4,'zl'=4,'x'=4,'c'=2,'mp'=2] {'y'}, dimensions={0} | all-to-all | bytes 1048576 | tf_op jit(solution)/shard_map/all_to_all | solution.py:97
  21.3 0.7 broadcast_in_dim.13
  22.0 12.8 %all-to-all-start = ((s32[128,4,65]{2,1,0:T(4,128)}), s32[128,4,65]{2,1,0:T(4,128)S(1)}, u32[]{:S(2)}, u32[]{:S(2)}) async-start(s32[128,4,65]{2,1,0:T(4,128)} %broadcast_in_dim.13), calls=%async_computation | async-start | bytes 524288 | tf_op jit(solution)/shard_map/all_to_all | solution.py:85
  34.9 15.7 %copy.59 = bf16[28,76032]{0,1:T(8,128)(2,1)} copy(bf16[28,76032]{1,0:T(8,128)(2,1)} %param.16) | data formatting | bytes 8515584 | tf_op args[2]
  52.0 64.8 %gather_fusion = bf16[16384,28]{1,0:T(8,128)(2,1)} fusion(bf16[28,76032]{0,1:T(8,128)(2,1)} %copy.59, s32[16384]{0:T(1024)S(1)} %broadcast_clamp_fusion), kind=kCustom, calls=%fused_computation | custom fusion | bytes 1900544 | tf_op jit(solution)/shard_map/gather | solution.py:109
  116.8 3.8 %copy.63 = bf16[28,128,128]{2,0,1:T(8,128)(2,1)S(1)} copy(bf16[28,128,128]{0,2,1:T(8,128)(2,1)} %bitcast.97) | data formatting | bytes 1835008 | tf_op jit(solution)/shard_map/concatenate | solution.py:123
  120.9 41.0 %all_to_all.24 = bf16[30,128,128]{2,0,1:T(8,128)(2,1)S(1)} all-to-all(bf16[30,128,128]{2,0,1:T(8,128)(2,1)S(1)} %pad_maximum_fusion), channel_id=1, replica_groups=mesh['y'=4,'zl'=4,'x'=4,'c'=2,'mp'=2] {'y','zl','x','c'}, dimensions={1} | all-to-all | bytes 1966080 | tf_op jit(solution)/shard_map/all_to_all | solution.py:124
  161.9 1.3 copy.64
  163.3 4.4 %collective-permute-start = (bf16[128,28,128]{0,2,1:T(8,128)(2,1)S(1)}, bf16[128,28,128]{0,2,1:T(8,128)(2,1)}, u32[]{:S(2)}, u32[]{:S(2)}) collective-permute-start(bf16[128,28,128]{0,2,1:T(8,128)(2,1)S(1)} %slice.76), channel_id=1, source_target_pairs={{0,1},{1,0},{2,3},{3,2},{4,5},{5,4},{6,7},{7,6},{8,9},{9,8},{10,11... | collective-permute-start | bytes 2752520 | tf_op jit(solution)/shard_map/ppermute | solution.py:129
  169.2 38.7 %collective-permute-done = bf16[128,28,128]{0,2,1:T(8,128)(2,1)} collective-permute-done((bf16[128,28,128]{0,2,1:T(8,128)(2,1)S(1)}, bf16[128,28,128]{0,2,1:T(8,128)(2,1)}, u32[]{:S(2)}, u32[]{:S(2)}) %collective-permute-start) | collective-permute-done | bytes 917536 | tf_op jit(solution)/shard_map/ppermute | solution.py:129
  207.9 2.1 fusion.3
  210.1 2.3 fusion.6
  212.4 8.0 %slice.78 = bf16[128,28,1152]{2,1,0:T(8,128)(2,1)} slice(bf16[128,32,2048]{2,1,0:T(8,128)(2,1)} %bitcast.89), slice={[0:128], [0:28], [0:1152]} | slice | bytes 16515072 | tf_op jit(solution)/shard_map/slice | solution.py:100
  220.4 9.6 %fusion = f32[256,1152,1]{1,0,2:T(8,128)S(1)} fusion(bf16[128,28,1152]{2,1,0:T(8,128)(2,1)} %slice.78, f32[128,28]{0,1:T(8,128)S(1)} %copy.66, f32[256]{0:T(256)S(1)} %add_rsqrt_fusion, bf16[128,28,128]{0,2,1:T(8,128)(2,1)} %collective-permute-done, bf16[128,28,128]{0,2,1:T(8,128)(2,1)S(1)} %slice.76, pred[]{:T(512)S(6)} %eq.3), kind=kOutput, calls=%fused_computation.1 | convolution fusion | flops 2125856768 | bytes 11287553 | tf_op jit(solution)/shard_map/abt,abn->tn/dot_general | solution.py:141
  230.2 1.0 slice.83
  231.2 0.7 slice_bitcast_fusion.1
  231.9 1.3 reshape.204
  237.5 3.9 %slice.77 = bf16[128,28,896]{2,1,0:T(8,128)(2,1)S(1)} slice(bf16[128,32,2048]{2,1,0:T(8,128)(2,1)} %bitcast.90), slice={[0:128], [0:28], [1152:2048]} | slice | bytes 12845056 | tf_op jit(solution)/shard_map/slice | solution.py:101
  241.6 4.4 %multiply_add_fusion = f32[128,28,4,64]{0,3,2,1:T(8,128)S(1)} fusion(bf16[4,64,896,1]{2,1,0,3:T(8,128)(2,1)S(1)} %reshape.228, bf16[128,28,896]{2,1,0:T(8,128)(2,1)S(1)} %slice.77, f32[4,64]{1,0:T(4,128)S(1)} %bitcast.112, f32[128,28,4]{0,2,1:T(4,128)S(1)} %copy.72), kind=kOutput, calls=%fused_computation.10 | convolution fusion | flops 1646919680 | bytes 10609664 | tf_op jit(solution)/shard_map/tc,abc->abt/dot_general | solution.py:171
  246.0 1.8 copy-done
  247.8 1.1 fusion.24
  248.9 4.9 %collective-permute-start.1 = (bf16[128,28,128]{0,2,1:T(8,128)(2,1)}, bf16[128,28,128]{0,2,1:T(8,128)(2,1)}, u32[]{:S(2)}, u32[]{:S(2)}) collective-permute-start(bf16[128,28,128]{0,2,1:T(8,128)(2,1)} %fusion.24), channel_id=1, source_target_pairs={{0,1},{1,0},{2,3},{3,2},{4,5},{5,4},{6,7},{7,6},{8,9},{9,8},{10,11... | collective-permute-start | bytes 2752520 | tf_op jit(solution)/shard_map/ppermute | solution.py:181
  254.0 0.8 fusion.32
  258.2 2.3 slice.90
  260.5 2.9 slice.92
  263.7 1.6 reshape.211
  265.4 1.4 convolution_multiply_fusion.2
  266.7 1.5 convolution_multiply_fusion
  268.2 25.6 %collective-permute-done.1 = bf16[128,28,128]{0,2,1:T(8,128)(2,1)} collective-permute-done((bf16[128,28,128]{0,2,1:T(8,128)(2,1)}, bf16[128,28,128]{0,2,1:T(8,128)(2,1)}, u32[]{:S(2)}, u32[]{:S(2)}) %collective-permute-start.1) | collective-permute-done | bytes 917536 | tf_op jit(solution)/shard_map/ppermute | solution.py:181
  293.8 2.2 multiply_reduce_fusion.1
  296.1 1.8 multiply_reduce_fusion
  (82 shorter events, 9.9 us)
Async XLA Ops:
  7.2 13.9 %copy-start.14 = (s32[4]{0:T(128)S(1)}, s32[4]{0:T(128)}, u32[]{:S(2)}) copy-start(s32[4]{0:T(128)} %param.15) | copy-start | bytes 52
  7.2 14.0 %copy-start.13 = (s32[4,64]{1,0:T(4,128)S(1)}, s32[4,64]{1,0:T(4,128)}, u32[]{:S(2)}) copy-start(s32[4,64]{1,0:T(4,128)} %param.14) | copy-start | bytes 3076
  7.2 205.2 %all-gather.3.cloned.1.call-start = ((), (), s32[]{:S(2)}) async-start(), calls=%async_computation.3 | async-start | bytes 17301504 | tf_op jit(solution)/shard_map/all_gather | solution.py:98
  22.0 29.7 %all-to-all-start = ((s32[128,4,65]{2,1,0:T(4,128)}), s32[128,4,65]{2,1,0:T(4,128)S(1)}, u32[]{:S(2)}, u32[]{:S(2)}) async-start(s32[128,4,65]{2,1,0:T(4,128)} %broadcast_in_dim.13), calls=%async_computation | async-start | bytes 524288 | tf_op jit(solution)/shard_map/all_to_all | solution.py:85
  34.9 15.7 %copy-start.8 = (bf16[4,3584]{1,0:T(4,128)(2,1)S(1)}, bf16[4,3584]{1,0:T(4,128)(2,1)}, u32[]{:S(2)}) copy-start(bf16[4,3584]{1,0:T(4,128)(2,1)} %param.25) | copy-start | bytes 86020
  34.9 16.2 %copy-start.5 = (bf16[4,3584]{1,0:T(4,128)(2,1)S(1)}, bf16[4,3584]{1,0:T(4,128)(2,1)}, u32[]{:S(2)}) copy-start(bf16[4,3584]{1,0:T(4,128)(2,1)} %param.22) | copy-start | bytes 86020
  161.9 6.1 %copy-start.6 = (bf16[4,1152]{1,0:T(4,128)(2,1)S(1)}, bf16[4,1152]{1,0:T(4,128)(2,1)}, u32[]{:S(2)}) copy-start(bf16[4,1152]{1,0:T(4,128)(2,1)} %param.23) | copy-start | bytes 27652
  161.9 6.2 %copy-start.9 = (f32[3584]{0:T(1024)S(1)}, f32[3584]{0:T(1024)}, u32[]{:S(2)}) copy-start(f32[3584]{0:T(1024)} %param.17) | copy-start | bytes 43012
  163.3 44.6 %collective-permute-start = (bf16[128,28,128]{0,2,1:T(8,128)(2,1)S(1)}, bf16[128,28,128]{0,2,1:T(8,128)(2,1)}, u32[]{:S(2)}, u32[]{:S(2)}) collective-permute-start(bf16[128,28,128]{0,2,1:T(8,128)(2,1)S(1)} %slice.76), channel_id=1, source_target_pairs={{0,1},{1,0},{2,3},{3,2},{4,5},{5,4},{6,7},{7,6},{8,9},{9,8},{10,11... | collective-permute-start | bytes 2752520 | tf_op jit(solution)/shard_map/ppermute | solution.py:129
  220.4 9.6 %copy-start.11 = (f32[1152]{0:T(1024)S(1)}, f32[1152]{0:T(1024)}, u32[]{:S(2)}) copy-start(f32[1152]{0:T(1024)} %param.19) | copy-start | bytes 13828
  233.2 0.9 copy-start.2
  233.2 1.0 copy-start.3
  233.2 1.0 copy-start.4
  234.2 0.7 copy-start.7
  237.4 3.9 %copy-start.12 = (bf16[4,896]{1,0:T(4,128)(2,1)S(1)}, bf16[4,896]{1,0:T(4,128)(2,1)}, u32[]{:S(2)}) copy-start(bf16[4,896]{1,0:T(4,128)(2,1)} %param.24) | copy-start | bytes 21508
  246.0 1.8 copy-start
  246.0 7.8 %copy-start.10 = (f32[3584]{0:T(1024)S(1)}, f32[3584]{0:T(1024)}, u32[]{:S(2)}) copy-start(f32[3584]{0:T(1024)} %param.21) | copy-start | bytes 43012
  248.9 44.9 %collective-permute-start.1 = (bf16[128,28,128]{0,2,1:T(8,128)(2,1)}, bf16[128,28,128]{0,2,1:T(8,128)(2,1)}, u32[]{:S(2)}, u32[]{:S(2)}) collective-permute-start(bf16[128,28,128]{0,2,1:T(8,128)(2,1)} %fusion.24), channel_id=1, source_target_pairs={{0,1},{1,0},{2,3},{3,2},{4,5},{5,4},{6,7},{7,6},{8,9},{9,8},{10,11... | collective-permute-start | bytes 2752520 | tf_op jit(solution)/shard_map/ppermute | solution.py:181
  268.2 27.9 %copy-start.1 = (f32[128,28,4,64]{0,3,2,1:T(8,128)S(1)}, f32[128,28,4,64]{0,3,2,1:T(8,128)}, u32[]{:S(2)}) copy-start(f32[128,28,4,64]{0,3,2,1:T(8,128)} %copy-done) | copy-start | bytes 11010052
Sparse Core Ops, SparseCore 0:
  21.2 105.9 all-gather.2

commit v8 on v7

--- a/solution.py
+++ b/solution.py
@@ -92,21 +92,20 @@
         ],
         axis=0,
     )
-    y_count = lax.axis_size("y")
-    spread_rows = jnp.broadcast_to(stacked[None], (y_count,) + stacked.shape)
-    gathered = lax.all_to_all(spread_rows, "y", split_axis=0, concat_axis=0, tiled=True)
-    gathered = lax.all_gather(gathered, BLOCK_AXES, axis=1)
+    block_gathered = lax.all_gather(stacked, BLOCK_AXES, axis=0)
+    mp_index = lax.axis_index("mp")
+    share = members // mp_size
+    half_ids = lax.dynamic_slice_in_dim(
+        all_ids.reshape(member_count, members, length), mp_index * share, share, 1
+    )
+    picked = embed_table.at[:, half_ids.reshape(-1)].get(mode="promise_in_bounds")
+    after_pick = picked[0, 0] * jnp.zeros((), picked.dtype)
+    gathered = lax.all_gather(block_gathered + after_pick, "y", axis=0)
     gathered = gathered.reshape((member_count,) + stacked.shape)
     block_qkv = gathered[:, :feature_rows, :qkv_cols]
     block_out = gathered[:, :feature_rows, qkv_cols:]
     right_cols = gathered[:, feature_rows:, :qkv_cols].reshape(population, qkv_cols)
     left_cols = gathered[:, feature_rows:, qkv_cols:].reshape(population, out_cols)
-    mp_index = lax.axis_index("mp")
-    share = members // mp_size
-    half_ids = lax.dynamic_slice_in_dim(
-        all_ids.reshape(member_count, members, length), mp_index * share, share, 1
-    )
-    picked = embed_table.at[:, half_ids.reshape(-1)].get(mode="promise_in_bounds")
     token_block = share * length
     factor_width = 2 * feature_rows * members
     factor_rows = -(-factor_width // token_block)

time: 307 us -> 360 us (1.17)
  the two profiles are of different devices: /device:TPU:1 before, /device:TPU:36 now
where the time goes in v8:
time: 360 us; the launch traced here: 359 us
  waiting for transfers between devices  138 us (38%)
  local copies, waits for them, and re-layouts  110 us (31%)
  blocking collectives  38.9 us (11%)
  starting transfers between devices  21.7 us (6%)
  matrix products  18.2 us (5%)
  between operations  17.8 us (5%)
  other arithmetic  14.4 us (4%)
    all_gather x1, waiting for transfers between devices, on_device(): gathered = lax.all_gather(block_gathered + after_pick, 'y', axis=0)  71.4 us
    gather x1, local copies, waits for them, and re-layouts, on_device(): embed_table.at[:, half_ids.reshape(-1)].get(mode='promise_in_bounds')  64.2 us
    ppermute x1, waiting for transfers between devices, on_device(): other_half = lax.ppermute(own_half, 'mp', perm=[(0, 1), (1, 0)])  39.2 us
    all_to_all x1, blocking collectives, on_device(): lax.all_to_all(combined, MEMBER, split_axis=1, concat_axis=0, tiled=True)  38.9 us
    ppermute x1, waiting for transfers between devices, on_device(): lax.ppermute(sent_term.astype(jnp.bfloat16), 'mp', perm=[(0, 1), (1, 0)])  27.4 us
    unnamed x28, local copies, waits for them, and re-layouts  19.2 us
    all_to_all x1, starting transfers between devices, on_device(): lax.all_to_all(spread_ids, MEMBER, split_axis=0, concat_axis=0, tiled=True)  12.4 us
  transfers between devices with their start and end apart: 5, of which 3 were waited for; matrix products, arithmetic and copies ran while one was open for 30% of the time, Pallas kernels for 0%

profile of v8, /device:TPU:36, one launch (start us, length us, event | category | flops | bytes accessed | tf_op | source)
XLA Modules:
  0.0 358.8 jit_solution(9151870323961963763)
XLA Ops:
  7.2 1.6 maximum_maximum_fusion
  11.1 12.4 %all-to-all-start = ((s32[128,4,65]{2,1,0:T(4,128)}), s32[128,4,65]{2,1,0:T(4,128)S(1)}, u32[]{:S(2)}, u32[]{:S(2)}) async-start(s32[128,4,65]{2,1,0:T(4,128)} %broadcast_in_dim.11), calls=%async_computation | async-start | bytes 524288 | tf_op jit(solution)/shard_map/all_to_all | solution.py:85
  23.6 15.7 %copy.61 = bf16[28,76032]{0,1:T(8,128)(2,1)} copy(bf16[28,76032]{1,0:T(8,128)(2,1)} %param.16) | data formatting | bytes 8515584 | tf_op args[2]
  39.6 64.2 %gather_fusion = bf16[16384,28]{1,0:T(8,128)(2,1)} fusion(bf16[28,76032]{0,1:T(8,128)(2,1)} %copy.61, s32[16384]{0:T(1024)S(1)} %broadcast_clamp_fusion), kind=kCustom, calls=%fused_computation | custom fusion | bytes 1900544 | tf_op jit(solution)/shard_map/gather | solution.py:101
  103.8 1.2 slice.81
  105.7 2.5 broadcast_add_fusion
  108.1 4.2 %copy.67 = bf16[32,32,2048]{2,0,1:T(8,128)(2,1)} copy(bf16[32,32,2048]{2,1,0:T(8,128)(2,1)S(1)} %bitcast.90) | data formatting | bytes 8388608 | tf_op jit(solution)/shard_map/add | solution.py:103
  114.2 3.8 %copy.65 = bf16[28,128,128]{2,0,1:T(8,128)(2,1)S(1)} copy(bf16[28,128,128]{0,2,1:T(8,128)(2,1)} %bitcast.96) | data formatting | bytes 1835008 | tf_op jit(solution)/shard_map/concatenate | solution.py:122
  118.2 38.9 %all_to_all.18 = bf16[30,128,128]{2,0,1:T(8,128)(2,1)S(1)} all-to-all(bf16[30,128,128]{2,0,1:T(8,128)(2,1)S(1)} %pad_maximum_fusion), channel_id=1, replica_groups=mesh['y'=4,'zl'=4,'x'=4,'c'=2,'mp'=2] {'y','zl','x','c'}, dimensions={1} | all-to-all | bytes 1966080 | tf_op jit(solution)/shard_map/all_to_all | solution.py:123
  157.1 1.3 copy.66
  158.5 4.6 %collective-permute-start = (bf16[128,28,128]{0,2,1:T(8,128)(2,1)S(1)}, bf16[128,28,128]{0,2,1:T(8,128)(2,1)}, u32[]{:S(2)}, u32[]{:S(2)}) collective-permute-start(bf16[128,28,128]{0,2,1:T(8,128)(2,1)S(1)} %slice.80), channel_id=1, source_target_pairs={{0,1},{1,0},{2,3},{3,2},{4,5},{5,4},{6,7},{7,6},{8,9},{9,8},{10,11... | collective-permute-start | bytes 2752520 | tf_op jit(solution)/shard_map/ppermute | solution.py:128
  164.6 39.2 %collective-permute-done = bf16[128,28,128]{0,2,1:T(8,128)(2,1)} collective-permute-done((bf16[128,28,128]{0,2,1:T(8,128)(2,1)S(1)}, bf16[128,28,128]{0,2,1:T(8,128)(2,1)}, u32[]{:S(2)}, u32[]{:S(2)}) %collective-permute-start) | collective-permute-done | bytes 917536 | tf_op jit(solution)/shard_map/ppermute | solution.py:128
  203.7 2.2 fusion.3
  206.0 2.3 fusion.6
  208.3 71.4 %all-gather.7.cloned.1.call-done = bf16[128,32,2048]{2,0,1:T(8,128)(2,1)} async-done(((bf16[32,32,2048]{2,0,1:T(8,128)(2,1)}), bf16[128,32,2048]{2,0,1:T(8,128)(2,1)}) %all-gather.7.cloned.1.call-update) | async-done | bytes 16777232 | tf_op jit(solution)/shard_map/all_gather | solution.py:103
  279.7 6.6 %fusion = f32[256,1152,1]{1,0,2:T(8,128)S(1)} fusion(bf16[128,32,2048]{2,0,1:T(8,128)(2,1)} %all-gather.7.cloned.1.call-done, f32[128,28]{0,1:T(8,128)S(1)} %copy.68, f32[256]{0:T(256)S(1)} %add_rsqrt_fusion, bf16[128,28,128]{0,2,1:T(8,128)(2,1)} %collective-permute-done, bf16[128,28,128]{0,2,1:T(8,128)(2,1)S(1)} %slice.80, pred[]{:T(512)S(6)} %eq.3), kind=kOutput, calls=%fused_computation.1 | convolution fusion | flops 2125856768 | bytes 11287553 | tf_op jit(solution)/shard_map/abt,abn->tn/dot_general | solution.py:140
  286.5 1.0 slice.88
  288.2 1.3 reshape.205
  294.0 4.2 %multiply_add_fusion = f32[128,28,4,64]{0,3,2,1:T(8,128)S(1)} fusion(bf16[4,64,896,1]{2,1,0,3:T(8,128)(2,1)S(1)} %reshape.232, bf16[128,32,2048]{2,0,1:T(8,128)(2,1)} %all-gather.7.cloned.1.call-done, f32[4,64]{1,0:T(4,128)S(1)} %bitcast.111, f32[128,28,4]{0,2,1:T(4,128)S(1)} %copy.73), kind=kOutput, calls=%fused_computation.10 | convolution fusion | flops 1646919680 | bytes 10609664 | tf_op jit(solution)/shard_map/tc,abc->abt/dot_general | solution.py:170
  298.3 1.8 copy-done
  300.0 1.1 fusion.24
  301.1 4.6 %collective-permute-start.1 = (bf16[128,28,128]{0,2,1:T(8,128)(2,1)}, bf16[128,28,128]{0,2,1:T(8,128)(2,1)}, u32[]{:S(2)}, u32[]{:S(2)}) collective-permute-start(bf16[128,28,128]{0,2,1:T(8,128)(2,1)} %fusion.24), channel_id=1, source_target_pairs={{0,1},{1,0},{2,3},{3,2},{4,5},{5,4},{6,7},{7,6},{8,9},{9,8},{10,11... | collective-permute-start | bytes 2752520 | tf_op jit(solution)/shard_map/ppermute | solution.py:180
  305.9 0.8 fusion.32
  310.1 1.3 slice.97
  312.1 1.1 reshape.212
  313.2 1.4 slice.95
  314.6 0.9 copy.77
  315.8 2.6 convolution_multiply_fusion.2
  318.4 1.5 convolution_multiply_fusion
  319.8 27.4 %collective-permute-done.1 = bf16[128,28,128]{0,2,1:T(8,128)(2,1)} collective-permute-done((bf16[128,28,128]{0,2,1:T(8,128)(2,1)}, bf16[128,28,128]{0,2,1:T(8,128)(2,1)}, u32[]{:S(2)}, u32[]{:S(2)}) %collective-permute-start.1) | collective-permute-done | bytes 917536 | tf_op jit(solution)/shard_map/ppermute | solution.py:180
  347.3 2.2 multiply_reduce_fusion.1
  349.5 1.8 multiply_reduce_fusion
  (82 shorter events, 14.1 us)
Async XLA Ops:
  7.2 98.5 %all-gather.5.cloned.1.call-start = ((), (), s32[]{:S(2)}) async-start(), calls=%async_computation.2 | async-start | bytes 4325376 | tf_op jit(solution)/shard_map/all_gather | solution.py:95
  11.1 28.2 %all-to-all-start = ((s32[128,4,65]{2,1,0:T(4,128)}), s32[128,4,65]{2,1,0:T(4,128)S(1)}, u32[]{:S(2)}, u32[]{:S(2)}) async-start(s32[128,4,65]{2,1,0:T(4,128)} %broadcast_in_dim.11), calls=%async_computation | async-start | bytes 524288 | tf_op jit(solution)/shard_map/all_to_all | solution.py:85
  23.5 256.2 %all-gather.7.cloned.1.call-start = ((), (), s32[]{:S(2)}) async-start(), calls=%async_computation.3 | async-start | bytes 20971520 | tf_op jit(solution)/shard_map/all_gather | solution.py:103
  112.4 0.7 copy-start.8
  112.4 1.2 copy-start.5
  157.1 6.4 %copy-start.6 = (bf16[4,1152]{1,0:T(4,128)(2,1)S(1)}, bf16[4,1152]{1,0:T(4,128)(2,1)}, u32[]{:S(2)}) copy-start(bf16[4,1152]{1,0:T(4,128)(2,1)} %param.23) | copy-start | bytes 27652
  157.1 6.4 %copy-start.9 = (f32[3584]{0:T(1024)S(1)}, f32[3584]{0:T(1024)}, u32[]{:S(2)}) copy-start(f32[3584]{0:T(1024)} %param.17) | copy-start | bytes 43012
  158.5 45.3 %collective-permute-start = (bf16[128,28,128]{0,2,1:T(8,128)(2,1)S(1)}, bf16[128,28,128]{0,2,1:T(8,128)(2,1)}, u32[]{:S(2)}, u32[]{:S(2)}) collective-permute-start(bf16[128,28,128]{0,2,1:T(8,128)(2,1)S(1)} %slice.80), channel_id=1, source_target_pairs={{0,1},{1,0},{2,3},{3,2},{4,5},{5,4},{6,7},{7,6},{8,9},{9,8},{10,11... | collective-permute-start | bytes 2752520 | tf_op jit(solution)/shard_map/ppermute | solution.py:128
  208.3 78.0 %copy-start.11 = (f32[1152]{0:T(1024)S(1)}, f32[1152]{0:T(1024)}, u32[]{:S(2)}) copy-start(f32[1152]{0:T(1024)} %param.19) | copy-start | bytes 13828
  289.5 0.9 copy-start.2
  289.5 1.0 copy-start.3
  289.5 1.0 copy-start.4
  290.5 0.7 copy-start.7
  292.3 1.4 copy-start.12
  298.2 1.8 copy-start
  298.3 7.5 %copy-start.10 = (f32[3584]{0:T(1024)S(1)}, f32[3584]{0:T(1024)}, u32[]{:S(2)}) copy-start(f32[3584]{0:T(1024)} %param.21) | copy-start | bytes 43012
  301.1 46.1 %collective-permute-start.1 = (bf16[128,28,128]{0,2,1:T(8,128)(2,1)}, bf16[128,28,128]{0,2,1:T(8,128)(2,1)}, u32[]{:S(2)}, u32[]{:S(2)}) collective-permute-start(bf16[128,28,128]{0,2,1:T(8,128)(2,1)} %fusion.24), channel_id=1, source_target_pairs={{0,1},{1,0},{2,3},{3,2},{4,5},{5,4},{6,7},{7,6},{8,9},{9,8},{10,11... | collective-permute-start | bytes 2752520 | tf_op jit(solution)/shard_map/ppermute | solution.py:180
  319.8 29.7 %copy-start.1 = (f32[128,28,4,64]{0,3,2,1:T(8,128)S(1)}, f32[128,28,4,64]{0,3,2,1:T(8,128)}, u32[]{:S(2)}) copy-start(f32[128,28,4,64]{0,3,2,1:T(8,128)} %copy-done) | copy-start | bytes 11010052
Sparse Core Ops, SparseCore 0:
  10.4 65.3 all-gather.4
  112.5 167.1 all-gather.6

commit v9 on v7

--- a/solution.py
+++ b/solution.py
@@ -126,7 +126,8 @@
     own_half = arrived[:, :feature_rows, :]
     factor_cols = arrived[:, feature_rows:, :].reshape(member_count, factor_rows * token_block)
     factor_cols = factor_cols[:, :factor_width].reshape(population, 2 * feature_rows)
-    other_half = lax.ppermute(own_half, "mp", perm=[(0, 1), (1, 0)])
+    weights_ready = gathered[0, 0, 0] * jnp.zeros((), gathered.dtype)
+    other_half = lax.ppermute(own_half + weights_ready, "mp", perm=[(0, 1), (1, 0)])
     embedded = jnp.where(
         mp_index == 0,
         jnp.concatenate([own_half, other_half], axis=2),

time: 307 us -> 301 us (0.980)
  waiting for transfers between devices: 64.4 us -> 50 us
  local copies, waits for them, and re-layouts: 117 us -> 123 us
    ppermute x1, waiting for transfers between devices: 38.7 us -> 24.5 us  [on_device(): lax.ppermute(own_half + weights_ready, 'mp', perm=[(0, 1), (1, 0)])]
    dot_general x1, matrix products: 4.42 us -> 7.5 us  [on_device(): jnp.einsum('tc,abc->abt', flat_context, block_out, preferred_element_type...]
    unnamed x32 -> x34, local copies, waits for them, and re-layouts: 18.4 us -> 20.3 us
  transfers between devices with their start and end apart: 4 -> 4, of which waited for: 2 -> 2; matrix products, arithmetic and copies ran while one was open for 35% -> 39% of each run, Pallas kernels for 0% -> 0%
where the time goes in v9:
time: 301 us; the launch traced here: 300 us
  local copies, waits for them, and re-layouts  123 us (41%)
  blocking collectives  53.8 us (18%)
  waiting for transfers between devices  50 us (17%)
  starting transfers between devices  21.9 us (7%)
  matrix products  21.4 us (7%)
  between operations  17.8 us (6%)
  other arithmetic  11.8 us (4%)
    gather x1, local copies, waits for them, and re-layouts, on_device(): embed_table.at[:, half_ids.reshape(-1)].get(mode='promise_in_bounds')  64.8 us
    all_to_all x1, blocking collectives, on_device(): lax.all_to_all(combined, MEMBER, split_axis=1, concat_axis=0, tiled=True)  41 us
    ppermute x1, waiting for transfers between devices, on_device(): lax.ppermute(sent_term.astype(jnp.bfloat16), 'mp', perm=[(0, 1), (1, 0)])  25.5 us
    ppermute x1, waiting for transfers between devices, on_device(): lax.ppermute(own_half + weights_ready, 'mp', perm=[(0, 1), (1, 0)])  24.5 us
    unnamed x34, local copies, waits for them, and re-layouts  20.3 us
    all_to_all x1, starting transfers between devices, on_device(): lax.all_to_all(spread_ids, MEMBER, split_axis=0, concat_axis=0, tiled=True)  12.8 us
    all_to_all x1, blocking collectives, on_device(): lax.all_to_all(spread_rows, 'y', split_axis=0, concat_axis=0, tiled=True)  12.8 us
    slice x1, local copies, waits for them, and re-layouts, on_device(): block_qkv = gathered[:, :feature_rows, :qkv_cols]  8.03 us
  transfers between devices with their start and end apart: 4, of which 2 were waited for; matrix products, arithmetic and copies ran while one was open for 39% of the time, Pallas kernels for 0%

profile of v9, /device:TPU:1, one launch (start us, length us, event | category | flops | bytes accessed | tf_op | source)
XLA Modules:
  0.0 299.5 jit_solution(4351879588014926365)
XLA Ops:
  7.2 1.0 maximum_maximum_fusion
  8.3 12.8 %all_to_all.23 = bf16[4,32,2048]{2,1,0:T(8,128)(2,1)} all-to-all(bf16[4,32,2048]{2,1,0:T(8,128)(2,1)S(1)} %broadcast_in_dim.14), channel_id=1, replica_groups=mesh['y'=4,'zl'=4,'x'=4,'c'=2,'mp'=2] {'y'}, dimensions={0} | all-to-all | bytes 1048576 | tf_op jit(solution)/shard_map/all_to_all | solution.py:97
  22.0 12.8 %all-to-all-start = ((s32[128,4,65]{2,1,0:T(4,128)}), s32[128,4,65]{2,1,0:T(4,128)S(1)}, u32[]{:S(2)}, u32[]{:S(2)}) async-start(s32[128,4,65]{2,1,0:T(4,128)} %broadcast_in_dim.13), calls=%async_computation | async-start | bytes 524288 | tf_op jit(solution)/shard_map/all_to_all | solution.py:85
  34.9 15.7 %copy.59 = bf16[28,76032]{0,1:T(8,128)(2,1)} copy(bf16[28,76032]{1,0:T(8,128)(2,1)} %param.16) | data formatting | bytes 8515584 | tf_op args[2]
  52.0 64.8 %gather_fusion = bf16[16384,28]{1,0:T(8,128)(2,1)} fusion(bf16[28,76032]{0,1:T(8,128)(2,1)} %copy.59, s32[16384]{0:T(1024)S(1)} %broadcast_clamp_fusion), kind=kCustom, calls=%fused_computation | custom fusion | bytes 1900544 | tf_op jit(solution)/shard_map/gather | solution.py:109
  116.9 3.8 %copy.63 = bf16[28,128,128]{2,0,1:T(8,128)(2,1)S(1)} copy(bf16[28,128,128]{0,2,1:T(8,128)(2,1)} %bitcast.99) | data formatting | bytes 1835008 | tf_op jit(solution)/shard_map/concatenate | solution.py:123
  120.9 41.0 %all_to_all.24 = bf16[30,128,128]{2,0,1:T(8,128)(2,1)S(1)} all-to-all(bf16[30,128,128]{2,0,1:T(8,128)(2,1)S(1)} %pad_maximum_fusion), channel_id=1, replica_groups=mesh['y'=4,'zl'=4,'x'=4,'c'=2,'mp'=2] {'y','zl','x','c'}, dimensions={1} | all-to-all | bytes 1966080 | tf_op jit(solution)/shard_map/all_to_all | solution.py:124
  161.9 1.3 copy.64
  163.3 1.2 slice.82
  165.1 1.1 broadcast_add_fusion
  166.2 4.2 %collective-permute-start = (bf16[128,28,128]{0,2,1:T(8,128)(2,1)}, bf16[128,28,128]{0,2,1:T(8,128)(2,1)}, u32[]{:S(2)}, u32[]{:S(2)}) collective-permute-start(bf16[128,28,128]{0,2,1:T(8,128)(2,1)} %get-tuple-element.7), channel_id=1, source_target_pairs={{0,1},{1,0},{2,3},{3,2},{4,5},{5,4},{6,7},{7,6},{8,9},{9,8},{10,11... | collective-permute-start | bytes 2752520 | tf_op jit(solution)/shard_map/ppermute | solution.py:130
  171.8 8.0 %slice.83 = bf16[128,28,1152]{2,1,0:T(8,128)(2,1)} slice(bf16[128,32,2048]{2,1,0:T(8,128)(2,1)} %bitcast.91), slice={[0:128], [0:28], [0:1152]} | slice | bytes 16515072 | tf_op jit(solution)/shard_map/slice | solution.py:100
  179.8 6.6 %slice.81 = bf16[128,28,896]{2,1,0:T(8,128)(2,1)} slice(bf16[128,32,2048]{2,1,0:T(8,128)(2,1)} %bitcast.92), slice={[0:128], [0:28], [1152:2048]} | slice | bytes 12845056 | tf_op jit(solution)/shard_map/slice | solution.py:101
  186.4 24.5 %collective-permute-done = bf16[128,28,128]{0,2,1:T(8,128)(2,1)} collective-permute-done((bf16[128,28,128]{0,2,1:T(8,128)(2,1)}, bf16[128,28,128]{0,2,1:T(8,128)(2,1)}, u32[]{:S(2)}, u32[]{:S(2)}) %collective-permute-start) | collective-permute-done | bytes 917536 | tf_op jit(solution)/shard_map/ppermute | solution.py:130
  210.9 2.3 fusion.3
  213.3 2.4 fusion.6
  215.7 1.8 copy-done
  217.5 7.5 %fusion = f32[256,1152,1]{1,0,2:T(8,128)S(1)} fusion(bf16[128,28,1152]{2,1,0:T(8,128)(2,1)S(1)} %copy-done, f32[128,28]{0,1:T(8,128)S(1)} %copy.66, f32[256]{0:T(256)S(1)} %add_rsqrt_fusion, bf16[128,28,128]{0,2,1:T(8,128)(2,1)} %collective-permute-done, bf16[128,28,128]{0,2,1:T(8,128)(2,1)S(1)} %get-tuple-element.8, pred[]{:T(512)S(6)} %eq.3), kind=kOutput, calls=%fused_computation.1 | convolution fusion | flops 2125856768 | bytes 11287553 | tf_op jit(solution)/shard_map/abt,abn->tn/dot_general | solution.py:142
  225.2 1.0 slice.88
  226.9 1.3 reshape.206
  232.9 7.5 %multiply_add_fusion = f32[128,28,4,64]{0,3,2,1:T(8,128)S(1)} fusion(bf16[4,64,896,1]{2,1,0,3:T(8,128)(2,1)S(1)} %reshape.230, bf16[128,28,896]{2,1,0:T(8,128)(2,1)} %slice.81, f32[4,64]{1,0:T(4,128)S(1)} %bitcast.114, f32[128,28,4]{0,2,1:T(4,128)S(1)} %copy.72), kind=kOutput, calls=%fused_computation.10 | convolution fusion | flops 1646919680 | bytes 10609664 | tf_op jit(solution)/shard_map/tc,abc->abt/dot_general | solution.py:172
  240.5 1.8 copy-done.1
  242.2 1.1 fusion.24
  243.3 4.8 %collective-permute-start.1 = (bf16[128,28,128]{0,2,1:T(8,128)(2,1)}, bf16[128,28,128]{0,2,1:T(8,128)(2,1)}, u32[]{:S(2)}, u32[]{:S(2)}) collective-permute-start(bf16[128,28,128]{0,2,1:T(8,128)(2,1)} %fusion.24), channel_id=1, source_target_pairs={{0,1},{1,0},{2,3},{3,2},{4,5},{5,4},{6,7},{7,6},{8,9},{9,8},{10,11... | collective-permute-start | bytes 2752520 | tf_op jit(solution)/shard_map/ppermute | solution.py:182
  252.5 2.3 slice.95
  254.8 2.9 slice.97
  258.0 1.6 reshape.213
  259.7 1.4 convolution_multiply_fusion.2
  261.0 1.5 convolution_multiply_fusion
  262.5 25.5 %collective-permute-done.1 = bf16[128,28,128]{0,2,1:T(8,128)(2,1)} collective-permute-done((bf16[128,28,128]{0,2,1:T(8,128)(2,1)}, bf16[128,28,128]{0,2,1:T(8,128)(2,1)}, u32[]{:S(2)}, u32[]{:S(2)}) %collective-permute-start.1) | collective-permute-done | bytes 917536 | tf_op jit(solution)/shard_map/ppermute | solution.py:182
  288.0 2.2 multiply_reduce_fusion.1
  290.3 1.8 multiply_reduce_fusion
  (85 shorter events, 12.3 us)
Async XLA Ops:
  7.2 13.9 %copy-start.15 = (s32[4]{0:T(128)S(1)}, s32[4]{0:T(128)}, u32[]{:S(2)}) copy-start(s32[4]{0:T(128)} %param.15) | copy-start | bytes 52
  7.2 14.0 %copy-start.14 = (s32[4,64]{1,0:T(4,128)S(1)}, s32[4,64]{1,0:T(4,128)}, u32[]{:S(2)}) copy-start(s32[4,64]{1,0:T(4,128)} %param.14) | copy-start | bytes 3076
  7.2 156.1 %all-gather.3.cloned.1.call-start = ((), (), s32[]{:S(2)}) async-start(), calls=%async_computation.3 | async-start | bytes 17301504 | tf_op jit(solution)/shard_map/all_gather | solution.py:98
  22.0 29.7 %all-to-all-start = ((s32[128,4,65]{2,1,0:T(4,128)}), s32[128,4,65]{2,1,0:T(4,128)S(1)}, u32[]{:S(2)}, u32[]{:S(2)}) async-start(s32[128,4,65]{2,1,0:T(4,128)} %broadcast_in_dim.13), calls=%async_computation | async-start | bytes 524288 | tf_op jit(solution)/shard_map/all_to_all | solution.py:85
  34.9 15.8 %copy-start.9 = (bf16[4,3584]{1,0:T(4,128)(2,1)S(1)}, bf16[4,3584]{1,0:T(4,128)(2,1)}, u32[]{:S(2)}) copy-start(bf16[4,3584]{1,0:T(4,128)(2,1)} %param.25) | copy-start | bytes 86020
  34.9 16.2 %copy-start.6 = (bf16[4,3584]{1,0:T(4,128)(2,1)S(1)}, bf16[4,3584]{1,0:T(4,128)(2,1)}, u32[]{:S(2)}) copy-start(bf16[4,3584]{1,0:T(4,128)(2,1)} %param.22) | copy-start | bytes 86020
  163.2 7.5 %copy-start.7 = (bf16[4,1152]{1,0:T(4,128)(2,1)S(1)}, bf16[4,1152]{1,0:T(4,128)(2,1)}, u32[]{:S(2)}) copy-start(bf16[4,1152]{1,0:T(4,128)(2,1)} %param.23) | copy-start | bytes 27652
  163.2 7.5 %copy-start.10 = (f32[3584]{0:T(1024)S(1)}, f32[3584]{0:T(1024)}, u32[]{:S(2)}) copy-start(f32[3584]{0:T(1024)} %param.17) | copy-start | bytes 43012
  166.2 44.7 %collective-permute-start = (bf16[128,28,128]{0,2,1:T(8,128)(2,1)}, bf16[128,28,128]{0,2,1:T(8,128)(2,1)}, u32[]{:S(2)}, u32[]{:S(2)}) collective-permute-start(bf16[128,28,128]{0,2,1:T(8,128)(2,1)} %get-tuple-element.7), channel_id=1, source_target_pairs={{0,1},{1,0},{2,3},{3,2},{4,5},{5,4},{6,7},{7,6},{8,9},{9,8},{10,11... | collective-permute-start | bytes 2752520 | tf_op jit(solution)/shard_map/ppermute | solution.py:130
  213.3 4.2 %copy-start = (bf16[128,28,1152]{2,1,0:T(8,128)(2,1)S(1)}, bf16[128,28,1152]{2,1,0:T(8,128)(2,1)}, u32[]{:S(2)}) copy-start(bf16[128,28,1152]{2,1,0:T(8,128)(2,1)} %slice.83) | copy-start | bytes 24772612
  217.5 7.5 %copy-start.12 = (f32[1152]{0:T(1024)S(1)}, f32[1152]{0:T(1024)}, u32[]{:S(2)}) copy-start(f32[1152]{0:T(1024)} %param.19) | copy-start | bytes 13828
  228.2 0.9 copy-start.3
  228.2 1.0 copy-start.4
  228.2 1.0 copy-start.5
  229.2 0.7 copy-start.8
  231.0 1.6 copy-start.13
  240.4 1.8 copy-start.1
  240.4 7.7 %copy-start.11 = (f32[3584]{0:T(1024)S(1)}, f32[3584]{0:T(1024)}, u32[]{:S(2)}) copy-start(f32[3584]{0:T(1024)} %param.21) | copy-start | bytes 43012
  243.3 44.7 %collective-permute-start.1 = (bf16[128,28,128]{0,2,1:T(8,128)(2,1)}, bf16[128,28,128]{0,2,1:T(8,128)(2,1)}, u32[]{:S(2)}, u32[]{:S(2)}) collective-permute-start(bf16[128,28,128]{0,2,1:T(8,128)(2,1)} %fusion.24), channel_id=1, source_target_pairs={{0,1},{1,0},{2,3},{3,2},{4,5},{5,4},{6,7},{7,6},{8,9},{9,8},{10,11... | collective-permute-start | bytes 2752520 | tf_op jit(solution)/shard_map/ppermute | solution.py:182
  262.5 27.7 %copy-start.2 = (f32[128,28,4,64]{0,3,2,1:T(8,128)S(1)}, f32[128,28,4,64]{0,3,2,1:T(8,128)}, u32[]{:S(2)}) copy-start(f32[128,28,4,64]{0,3,2,1:T(8,128)} %copy-done.1) | copy-start | bytes 11010052
Sparse Core Ops, SparseCore 0:
  21.2 105.9 all-gather.2
